TPU v7x, 768 devices: a whole 4x8x12 slice. The times are simulated.
768 devices in a mesh: shard: 16 (over y, x_lo), replica: 48 (over z, x_hi, core).
Axes of the slice: x: 4 (x_hi: 2, x_lo: 2; x = x_hi * 2 + x_lo), y: 8, z: 12, core: 2. Of those that a mesh axis runs over, the one named last changes fastest.
Arguments:
- queries: bfloat16 [196608, 1024], P(('shard', 'replica')), may hold values from -24 to 24
- keys: bfloat16 [196608, 1024], P(('shard', 'replica')), may hold values from -6 to 6
- values: bfloat16 [196608, 1024], P(('shard', 'replica')), may hold values from -7 to 7
- positions: int32 [196608], P(('shard', 'replica')), may hold values from 0 to 255, as said below
- live: int32 [196608], P(('shard', 'replica')), may hold values from 0 to 1, as said below
- out_weight: bfloat16 [1024, 2048], P(None, 'shard'), may hold values from -0.1875 to 0.1875
- grad_out: bfloat16 [196608, 2048], P(('shard', 'replica')), may hold values from -6 to 6
Outputs:
- grad_queries: bfloat16 [196608, 1024], P(('shard', 'replica'))
- grad_keys: bfloat16 [196608, 1024], P(('shard', 'replica'))
- grad_values: bfloat16 [196608, 1024], P(('shard', 'replica'))
- grad_weight: float32 [1024, 2048], P(None, 'shard')
Inputs may be any that keep to these rules, and one draw needn't show every extreme that they name: `positions`: within each aligned block of 256 tokens every grid index occurs once. Tokens of grid index under 8 are always live.
All inputs are finite; a program needn't handle non-finite values.
Results may differ from a plain program's by a relative error of at most 0.04.
Values may be sent and summed in bfloat16 or wider, within the bound.
No kernel may reach another device: no remote copies, remote signals or barrier semaphores. Data moves between devices by JAX's collectives and lax.ppermute only.
A program may use at most 64 MiB of HBM per device.

v0:
```python
import math

import jax
import jax.numpy as jnp
from jax import lax
from jax.sharding import PartitionSpec as P

HEADS = 8
HEAD_DIM = 128
PATCHES = 64
SEQ = 256


def local(queries, keys, values, positions, live, out_weight, grad_out):
    tok_rows = queries.shape[0]
    seq_count = tok_rows // SEQ
    q_width = out_weight.shape[0]
    score_scale = 1.0 / math.sqrt(HEAD_DIM)
    grad_att32 = lax.dot_general(
        grad_out,
        lax.all_gather(out_weight, "shard", axis=1, tiled=True),
        (((1,), (1,)), ((), ())),
        preferred_element_type=jnp.float32,
    )
    grad_att = grad_att32.astype(jnp.bfloat16)
    query_h = queries.reshape(seq_count, SEQ, HEADS, HEAD_DIM)
    key_h = keys.reshape(seq_count, SEQ, HEADS, HEAD_DIM)
    value_h = values.reshape(seq_count, SEQ, HEADS, HEAD_DIM)
    grad_h = grad_att.reshape(seq_count, SEQ, HEADS, HEAD_DIM)
    grid_index = positions.reshape(seq_count, SEQ)
    alive = live.reshape(seq_count, SEQ)
    frames_of = grid_index // PATCHES
    patch_of = grid_index % PATCHES
    same_frame = frames_of[:, :, None] == frames_of[:, None, :]
    earlier = (patch_of[:, :, None] == patch_of[:, None, :]) & (
        frames_of[:, None, :] < frames_of[:, :, None]
    )
    itself = (jnp.arange(SEQ)[:, None] == jnp.arange(SEQ)[None, :])[None]
    allowed = itself | (alive[:, None, :] == 1) & (same_frame | earlier)
    scores = (
        jnp.einsum("bqhd,bkhd->bhqk", query_h, key_h, preferred_element_type=jnp.float32)
        * score_scale
    )
    scores = jnp.where(allowed[:, None], scores, -jnp.inf)
    top_score = jnp.max(scores, axis=-1, keepdims=True)
    expo = jnp.exp(scores - top_score)
    softmax_w = expo / jnp.sum(expo, axis=-1, keepdims=True)
    probs_bf = softmax_w.astype(jnp.bfloat16)
    attended = jnp.einsum(
        "bhqk,bkhd->bqhd", probs_bf, value_h, preferred_element_type=jnp.float32
    ).astype(jnp.bfloat16)
    attended_rows = attended.reshape(tok_rows, q_width)
    total_tokens = tok_rows * lax.axis_size("shard") * lax.axis_size("replica")
    partial_value = lax.dot_general(
        attended_rows, grad_out, (((0,), (0,)), ((), ())), preferred_element_type=jnp.float32
    ) / math.sqrt(total_tokens)
    sliced = lax.psum_scatter(
        partial_value.astype(jnp.bfloat16), "shard", scatter_dimension=1, tiled=True
    ).astype(jnp.float32)
    grad_weight = lax.psum(sliced, "replica")
    grad_probs = jnp.einsum("bqhd,bkhd->bhqk", grad_h, value_h, preferred_element_type=jnp.float32)
    row_delta = jnp.einsum("bqhd,bqhd->bhq", grad_h, attended, preferred_element_type=jnp.float32)
    scores_bf = (softmax_w * (grad_probs - row_delta[:, :, :, None]) * score_scale).astype(
        jnp.bfloat16
    )
    grad_q = jnp.einsum("bhqk,bkhd->bqhd", scores_bf, key_h, preferred_element_type=jnp.float32)
    grad_k = jnp.einsum("bhqk,bqhd->bkhd", scores_bf, query_h, preferred_element_type=jnp.float32)
    grad_v = jnp.einsum("bhqk,bqhd->bkhd", probs_bf, grad_h, preferred_element_type=jnp.float32)
    return (
        grad_q.astype(jnp.bfloat16).reshape(tok_rows, q_width),
        grad_k.astype(jnp.bfloat16).reshape(tok_rows, q_width),
        grad_v.astype(jnp.bfloat16).reshape(tok_rows, q_width),
        grad_weight,
    )


def solution(mesh):
    in_specs = (
        P(("shard", "replica"), None),
        P(("shard", "replica"), None),
        P(("shard", "replica"), None),
        P(("shard", "replica")),
        P(("shard", "replica")),
        P(None, "shard"),
        P(("shard", "replica"), None),
    )
    out_specs = (
        P(("shard", "replica"), None),
        P(("shard", "replica"), None),
        P(("shard", "replica"), None),
        P(None, "shard"),
    )
    return jax.shard_map(local, mesh=mesh, in_specs=in_specs, out_specs=out_specs, check_vma=False)
```

profile of v0, /device:TPU:1, one launch (start us, length us, event | category | flops | bytes accessed | tf_op | source)
XLA Modules:
  0.0 471.5 jit_solution(11451250288191706024)
XLA Ops:
  7.3 0.7 all-gather.2.cloned.1.call-update
  8.0 1.2 copy.57
  9.2 1.2 copy.56
  10.5 1.0 copy.58
  11.5 0.2 fusion.7
  11.7 2.2 fusion.14
  13.9 118.5 %all-gather.2.cloned.1.call-done = bf16[1024,2048]{1,0:T(8,128)(2,1)} async-done(((bf16[1024,128]{1,0:T(8,128)(2,1)}), bf16[1024,2048]{1,0:T(8,128)(2,1)}) %all-gather.2.cloned.1.call-update) | async-done | bytes 4194320 | tf_op jit(solution)/shard_map/all_gather | solution.py:21
  132.5 3.5 fusion.2
  136.1 0.1 bitcast_convert_fusion
  136.2 1.4 copy.50
  137.5 2.3 multiply_reduce_fusion
  139.9 3.2 multiply_convert_fusion
  143.1 6.4 %copy.54 = bf16[1024,2048]{0,1:T(8,128)(2,1)} copy(bf16[1024,2048]{1,0:T(8,128)(2,1)} %multiply_convert_fusion) | data formatting | bytes 8388608
  149.5 0.3 copy.38
  149.9 2.3 convolution_convert_fusion.2
  152.2 1.0 copy.42
  153.2 2.4 multiply_convert_fusion.1
  155.6 0.3 convolution_convert_fusion
  155.9 1.0 copy.40
  156.9 0.5 convolution_convert_fusion.3
  157.4 1.0 copy.41
  158.4 105.7 %reduce-scatter.4.cloned.1.call-done = bf16[128,1024]{1,0:T(8,128)(2,1)} async-done(((bf16[2048,1024]{1,0:T(8,128)(2,1)}), bf16[128,1024]{1,0:T(8,128)(2,1)}) %reduce-scatter.4.cloned.1.call-update) | async-done | bytes 262160
  264.1 1.1 copy.55
  265.2 199.4 %all-reduce.1 = f32[1024,128]{1,0:T(8,128)} all-reduce(bf16[1024,128]{1,0:T(8,128)(2,1)S(1)} %copy.55), channel_id=1, replica_groups=mesh['shard'=16,'replica'=48] {'replica'}, use_global_device_ids=true, to_apply=%region_3.4 | all-reduce | flops 131072 | bytes 786432 | tf_op jit(solution)/shard_map/psum | solution.py:60
  (22 shorter events, 0.2 us)
Async XLA Ops:
  7.2 125.3 %copy-start = (bf16[256,2048]{1,0:T(8,128)(2,1)S(1)}, bf16[256,2048]{1,0:T(8,128)(2,1)}, u32[]{:S(2)}) copy-start(bf16[256,2048]{1,0:T(8,128)(2,1)} %param.13) | copy-start | bytes 3145732
  7.2 3.3 copy-start.3
  7.2 4.3 copy-start.7
  7.2 4.3 copy-start.6
  7.2 125.3 %all-gather.2.cloned.1.call-start = ((), (), s32[]{:S(2)}) async-start(), calls=%async_computation.1 | async-start | bytes 4456448 | tf_op jit(solution)/shard_map/all_gather | solution.py:21
  7.9 256.2 %reduce-scatter.4.cloned.1.call-start = ((), (), s32[]{:S(2)}) async-start(), calls=%async_computation.2 | async-start | bytes 4456448
  10.5 3.4 copy-start.1
  149.9 2.3 copy-start.5
  149.9 3.3 copy-start.4
  153.2 2.4 copy-start.2
Sparse Core Ops, SparseCore 0:
  10.3 122.0 all-gather.1
  149.7 114.3 reduce-scatter.3
where the time goes:
time: 476 us; the launch traced here: 471 us
  waiting for transfers between devices  225 us (47%)
  blocking collectives  199 us (42%)
  matrix products  16.7 us (4%)
  local copies, waits for them, and re-layouts  15.8 us (3%)
  between operations  14.2 us (3%)
    psum x1, blocking collectives, local(): grad_weight = lax.psum(sliced, 'replica')  199 us
    all_gather x1, waiting for transfers between devices, local(): lax.all_gather(out_weight, 'shard', axis=1, tiled=True)  119 us
    unnamed x3, waiting for transfers between devices  106 us
    unnamed x23, local copies, waits for them, and re-layouts  12 us
  transfers between devices with their start and end apart: 2, of which 2 were waited for; matrix products, arithmetic and copies ran while one was open for 3% of the time, Pallas kernels for 0%

commit v1 on v0

--- a/solution.py
+++ b/solution.py
@@ -16,10 +16,18 @@
     seq_count = tok_rows // SEQ
     q_width = out_weight.shape[0]
     score_scale = 1.0 / math.sqrt(HEAD_DIM)
-    grad_att32 = lax.dot_general(
-        grad_out,
-        lax.all_gather(out_weight, "shard", axis=1, tiled=True),
-        (((1,), (1,)), ((), ())),
+    shard_count = lax.axis_size("shard")
+    weight_blocks = lax.all_to_all(
+        jnp.broadcast_to(out_weight[None], (shard_count,) + out_weight.shape),
+        "shard",
+        0,
+        0,
+        tiled=True,
+    )
+    grad_att32 = jnp.einsum(
+        "tjc,jrc->tr",
+        grad_out.reshape(tok_rows, shard_count, -1),
+        weight_blocks,
         preferred_element_type=jnp.float32,
     )
     grad_att = grad_att32.astype(jnp.bfloat16)
@@ -51,13 +59,32 @@
     ).astype(jnp.bfloat16)
     attended_rows = attended.reshape(tok_rows, q_width)
     total_tokens = tok_rows * lax.axis_size("shard") * lax.axis_size("replica")
-    partial_value = lax.dot_general(
-        attended_rows, grad_out, (((0,), (0,)), ((), ())), preferred_element_type=jnp.float32
-    ) / math.sqrt(total_tokens)
-    sliced = lax.psum_scatter(
-        partial_value.astype(jnp.bfloat16), "shard", scatter_dimension=1, tiled=True
-    ).astype(jnp.float32)
-    grad_weight = lax.psum(sliced, "replica")
+    term = (
+        jnp.einsum(
+            "tr,tjc->jrc",
+            attended_rows,
+            grad_out.reshape(tok_rows, shard_count, -1),
+            preferred_element_type=jnp.float32,
+        )
+        / math.sqrt(total_tokens)
+    ).astype(jnp.bfloat16)
+    arrived = lax.all_to_all(term, "shard", 0, 0, tiled=True)
+    shard_sum = jnp.sum(arrived.astype(jnp.float32), axis=0)
+    replicas = lax.axis_size("replica")
+    piece_rows = -(-q_width // replicas)
+    padded = jnp.pad(shard_sum, ((0, piece_rows * replicas - q_width), (0, 0)))
+    pieces = lax.all_to_all(
+        padded.reshape(replicas, piece_rows, -1), "replica", 0, 0, tiled=True
+    )
+    piece_sum = jnp.sum(pieces, axis=0)
+    gathered = lax.all_to_all(
+        jnp.broadcast_to(piece_sum[None], (replicas,) + piece_sum.shape),
+        "replica",
+        0,
+        0,
+        tiled=True,
+    )
+    grad_weight = gathered.reshape(replicas * piece_rows, -1)[:q_width]
     grad_probs = jnp.einsum("bqhd,bkhd->bhqk", grad_h, value_h, preferred_element_type=jnp.float32)
     row_delta = jnp.einsum("bqhd,bqhd->bhq", grad_h, attended, preferred_element_type=jnp.float32)
     scores_bf = (softmax_w * (grad_probs - row_delta[:, :, :, None]) * score_scale).astype(

time: 476 us -> 303 us (0.64)
  waiting for transfers between devices: 225 us -> 103 us
  blocking collectives: 199 us -> 152 us
  starting transfers between devices: 0.08 us -> 13.5 us
  between operations: 14.2 us -> 0.84 us
    psum x1 -> x0, blocking collectives: 199 us -> none  [local(): grad_weight = lax.psum(sliced, 'replica')]
    all_to_all x0 -> x2, blocking collectives: none -> 152 us  [the longest x1 101 us: local(): arrived = lax.all_to_all(term, 'shard', 0, 0, tiled=True)]
    all_gather x1 -> x0, waiting for transfers between devices: 119 us -> none  [local(): lax.all_gather(out_weight, 'shard', axis=1, tiled=True)]
    unnamed x3 -> x0, waiting for transfers between devices: 106 us -> none
    all_to_all x0 -> x2, waiting for transfers between devices: none -> 103 us  [the longest x1 87.8 us: local(): lax.all_to_all(jnp.broadcast_to(out_weight[None], (shard_count,) + out_we...]
    all_to_all x0 -> x2, starting transfers between devices: none -> 13.5 us  [the longest x1 8.86 us: local(): lax.all_to_all(jnp.broadcast_to(out_weight[None], (shard_count,) + out_we...]
    unnamed x23 -> x19, local copies, waits for them, and re-layouts: 12 us -> 6.6 us
  transfers between devices with their start and end apart: 2 -> 2, of which waited for: 2 -> 2; matrix products, arithmetic and copies ran while one was open for 3% -> 6% of each run, Pallas kernels for 0% -> 0%
where the time goes in v1:
time: 303 us; the launch traced here: 302 us
  blocking collectives  152 us (50%)
  waiting for transfers between devices  103 us (34%)
  matrix products  16.5 us (5%)
  local copies, waits for them, and re-layouts  15.8 us (5%)
  starting transfers between devices  13.5 us (4%)
    all_to_all x1, blocking collectives, local(): arrived = lax.all_to_all(term, 'shard', 0, 0, tiled=True)  101 us
    all_to_all x1, waiting for transfers between devices, local(): lax.all_to_all(jnp.broadcast_to(out_weight[None], (shard_count,) + out_we...  87.8 us
    all_to_all x1, blocking collectives, local(): lax.all_to_all(padded.reshape(replicas, piece_rows, -1), 'replica', 0, 0,...  50.6 us
    all_to_all x1, waiting for transfers between devices, local(): lax.all_to_all(jnp.broadcast_to(piece_sum[None], (replicas,) + piece_sum....  15.3 us
    all_to_all x1, starting transfers between devices, local(): lax.all_to_all(jnp.broadcast_to(out_weight[None], (shard_count,) + out_we...  8.86 us
    unnamed x19, local copies, waits for them, and re-layouts  6.6 us
  transfers between devices with their start and end apart: 2, of which 2 were waited for; matrix products, arithmetic and copies ran while one was open for 6% of the time, Pallas kernels for 0%

profile of v1, /device:TPU:1, one launch (start us, length us, event | category | flops | bytes accessed | tf_op | source)
XLA Modules:
  0.0 302.5 jit_solution(9761882786652573614)
XLA Ops:
  0.6 3.8 %broadcast_in_dim.14 = bf16[16,1024,128]{2,1,0:T(8,128)(2,1)} broadcast(bf16[1024,128]{1,0:T(8,128)(2,1)} %param.12), dimensions={1,2} | broadcast | bytes 4456448 | tf_op jit(solution)/shard_map/broadcast_in_dim | solution.py:21
  4.5 8.9 %all-to-all-start = ((bf16[16,1024,128]{2,1,0:T(8,128)(2,1)}), bf16[16,1024,128]{2,1,0:T(8,128)(2,1)}, u32[]{:S(2)}, u32[]{:S(2)}) async-start(bf16[16,1024,128]{2,1,0:T(8,128)(2,1)} %broadcast_in_dim.14), calls=%async_computation | async-start | bytes 8388608 | tf_op jit(solution)/shard_map/all_to_all | solution.py:20
  13.6 1.0 copy.60
  14.6 1.2 copy.59
  16.1 2.2 fusion.20
  18.3 87.8 %all-to-all-done = bf16[16,1024,128]{2,1,0:T(8,128)(2,1)} async-done(((bf16[16,1024,128]{2,1,0:T(8,128)(2,1)}), bf16[16,1024,128]{2,1,0:T(8,128)(2,1)}, u32[]{:S(2)}, u32[]{:S(2)}) %all-to-all-start) | async-done | bytes 4194336 | tf_op jit(solution)/shard_map/all_to_all | solution.py:20
  106.2 3.5 %fusion.4 = bf16[32,8,8,128]{3,1,2,0:T(8,128)(2,1)S(1)} fusion(bf16[16,1024,128]{2,1,0:T(8,128)(2,1)} %all-to-all-done, bf16[256,2048]{1,0:T(8,128)(2,1)S(1)} %copy-done), kind=kOutput, calls=%fused_computation.14 | convolution fusion | flops 1074003968 | bytes 5767168 | tf_op jit(solution)/shard_map/tjc,jrc->tr/dot_general | solution.py:27
  109.9 1.4 copy.54
  111.3 2.3 multiply_reduce_fusion
  113.6 1.3 fusion.1
  114.9 101.2 %all_to_all.20 = bf16[16,1024,128]{2,1,0:T(8,128)(2,1)S(1)} all-to-all(bf16[16,1024,128]{2,1,0:T(8,128)(2,1)S(1)} %fusion.1), channel_id=1, replica_groups=mesh['shard'=16,'replica'=48] {'shard'}, dimensions={0} | all-to-all | bytes 8388608 | tf_op jit(solution)/shard_map/all_to_all | solution.py:71
  216.7 50.6 %all_to_all.21 = f32[48,22,128]{2,1,0:T(8,128)S(1)} all-to-all(f32[48,22,128]{2,1,0:T(8,128)S(1)} %reshape.298), channel_id=1, replica_groups=mesh['shard'=16,'replica'=48] {'replica'}, dimensions={0} | all-to-all | bytes 1081344 | tf_op jit(solution)/shard_map/all_to_all | solution.py:76
  267.4 0.8 broadcast_in_dim.15
  268.3 4.6 %all-to-all-start.3 = ((f32[48,22,128]{2,1,0:T(8,128)}), f32[48,22,128]{2,1,0:T(8,128)S(1)}, u32[]{:S(2)}, u32[]{:S(2)}) async-start(f32[48,22,128]{2,1,0:T(8,128)} %broadcast_in_dim.15), calls=%async_computation.3 | async-start | bytes 1179648 | tf_op jit(solution)/shard_map/all_to_all | solution.py:80
  272.9 1.1 copy.41
  274.0 2.5 multiply_convert_fusion.1
  276.6 1.1 convolution_convert_fusion
  277.7 2.0 copy.44
  279.7 1.3 convolution_convert_fusion.3
  281.0 2.0 copy.45
  283.0 2.3 convolution_convert_fusion.2
  285.3 1.0 copy.46
  286.3 15.3 %all-to-all-done.3 = f32[48,22,128]{2,1,0:T(8,128)S(1)} async-done(((f32[48,22,128]{2,1,0:T(8,128)}), f32[48,22,128]{2,1,0:T(8,128)S(1)}, u32[]{:S(2)}, u32[]{:S(2)}) %all-to-all-start.3) | async-done | bytes 540704 | tf_op jit(solution)/shard_map/all_to_all | solution.py:80
  301.7 0.8 slice.4
  (25 shorter events, 1.4 us)
Async XLA Ops:
  0.6 105.6 %copy-start = (bf16[256,2048]{1,0:T(8,128)(2,1)S(1)}, bf16[256,2048]{1,0:T(8,128)(2,1)}, u32[]{:S(2)}) copy-start(bf16[256,2048]{1,0:T(8,128)(2,1)} %param.13) | copy-start | bytes 3145732
  4.5 8.9 %copy-start.3 = (bf16[256,1024]{1,0:T(8,128)(2,1)S(1)}, bf16[256,1024]{1,0:T(8,128)(2,1)}, u32[]{:S(2)}) copy-start(bf16[256,1024]{1,0:T(8,128)(2,1)} %param.8) | copy-start | bytes 1572868
  4.5 9.1 %copy-start.4 = (bf16[256,1024]{1,0:T(8,128)(2,1)S(1)}, bf16[256,1024]{1,0:T(8,128)(2,1)}, u32[]{:S(2)}) copy-start(bf16[256,1024]{1,0:T(8,128)(2,1)} %param.9) | copy-start | bytes 1572868
  4.5 101.7 %all-to-all-start = ((bf16[16,1024,128]{2,1,0:T(8,128)(2,1)}), bf16[16,1024,128]{2,1,0:T(8,128)(2,1)}, u32[]{:S(2)}, u32[]{:S(2)}) async-start(bf16[16,1024,128]{2,1,0:T(8,128)(2,1)} %broadcast_in_dim.14), calls=%async_computation | async-start | bytes 8388608 | tf_op jit(solution)/shard_map/all_to_all | solution.py:20
  13.4 2.5 copy-start.6
  13.4 2.5 copy-start.5
  13.6 4.7 %copy-start.1 = (bf16[256,1024]{0,1:T(8,128)(2,1)}, bf16[256,1024]{0,1:T(8,128)(2,1)S(1)}, u32[]{:S(2)}) copy-start(bf16[256,1024]{0,1:T(8,128)(2,1)S(1)} %copy.58) | copy-start | bytes 1572868
  268.3 33.4 %all-to-all-start.3 = ((f32[48,22,128]{2,1,0:T(8,128)}), f32[48,22,128]{2,1,0:T(8,128)S(1)}, u32[]{:S(2)}, u32[]{:S(2)}) async-start(f32[48,22,128]{2,1,0:T(8,128)} %broadcast_in_dim.15), calls=%async_computation.3 | async-start | bytes 1179648 | tf_op jit(solution)/shard_map/all_to_all | solution.py:80
  274.0 2.5 copy-start.2

commit v2 on v1

--- a/solution.py
+++ b/solution.py
@@ -3,6 +3,8 @@
 import jax
 import jax.numpy as jnp
 from jax import lax
+import numpy as np
+from jax.sharding import Mesh
 from jax.sharding import PartitionSpec as P
 
 HEADS = 8
@@ -17,19 +19,30 @@
     q_width = out_weight.shape[0]
     score_scale = 1.0 / math.sqrt(HEAD_DIM)
     shard_count = lax.axis_size("shard")
+    cores = lax.axis_size("core")
+    core = lax.axis_index("core")
+    part_rows = q_width // cores
+    weight_part = lax.dynamic_slice_in_dim(out_weight, core * part_rows, part_rows, axis=0)
     weight_blocks = lax.all_to_all(
-        jnp.broadcast_to(out_weight[None], (shard_count,) + out_weight.shape),
+        jnp.broadcast_to(weight_part[None], (shard_count,) + weight_part.shape),
         "shard",
         0,
         0,
         tiled=True,
     )
+    weight_all = lax.all_to_all(
+        jnp.broadcast_to(weight_blocks[None], (cores,) + weight_blocks.shape),
+        "core",
+        0,
+        0,
+        tiled=True,
+    )
     grad_att32 = jnp.einsum(
-        "tjc,jrc->tr",
+        "tjc,pjrc->tpr",
         grad_out.reshape(tok_rows, shard_count, -1),
-        weight_blocks,
+        weight_all,
         preferred_element_type=jnp.float32,
-    )
+    ).reshape(tok_rows, q_width)
     grad_att = grad_att32.astype(jnp.bfloat16)
     query_h = queries.reshape(seq_count, SEQ, HEADS, HEAD_DIM)
     key_h = keys.reshape(seq_count, SEQ, HEADS, HEAD_DIM)
@@ -58,7 +71,7 @@
         "bhqk,bkhd->bqhd", probs_bf, value_h, preferred_element_type=jnp.float32
     ).astype(jnp.bfloat16)
     attended_rows = attended.reshape(tok_rows, q_width)
-    total_tokens = tok_rows * lax.axis_size("shard") * lax.axis_size("replica")
+    total_tokens = tok_rows * lax.axis_size("shard") * lax.axis_size("rz") * lax.axis_size("core")
     term = (
         jnp.einsum(
             "tr,tjc->jrc",
@@ -68,23 +81,32 @@
         )
         / math.sqrt(total_tokens)
     ).astype(jnp.bfloat16)
-    arrived = lax.all_to_all(term, "shard", 0, 0, tiled=True)
+    pair = lax.all_to_all(
+        term.reshape(shard_count, cores, part_rows, -1), "core", 1, 1, tiled=True
+    )
+    pair_sum = jnp.sum(pair.astype(jnp.float32), axis=1).astype(jnp.bfloat16)
+    arrived = lax.all_to_all(pair_sum, "shard", 0, 0, tiled=True)
     shard_sum = jnp.sum(arrived.astype(jnp.float32), axis=0)
-    replicas = lax.axis_size("replica")
-    piece_rows = -(-q_width // replicas)
-    padded = jnp.pad(shard_sum, ((0, piece_rows * replicas - q_width), (0, 0)))
+    groups = lax.axis_size("rz")
+    piece_rows = -(-part_rows // groups)
+    padded = jnp.pad(shard_sum, ((0, piece_rows * groups - part_rows), (0, 0)))
     pieces = lax.all_to_all(
-        padded.reshape(replicas, piece_rows, -1), "replica", 0, 0, tiled=True
+        padded.reshape(groups, piece_rows, -1), "rz", 0, 0, tiled=True
     )
     piece_sum = jnp.sum(pieces, axis=0)
     gathered = lax.all_to_all(
-        jnp.broadcast_to(piece_sum[None], (replicas,) + piece_sum.shape),
-        "replica",
+        jnp.broadcast_to(piece_sum[None], (groups * cores,) + piece_sum.shape),
+        ("rz", "core"),
         0,
         0,
         tiled=True,
     )
-    grad_weight = gathered.reshape(replicas * piece_rows, -1)[:q_width]
+    grad_weight = (
+        gathered.reshape(groups, cores, piece_rows, -1)
+        .transpose(1, 0, 2, 3)
+        .reshape(cores, groups * piece_rows, -1)[:, :part_rows]
+        .reshape(q_width, -1)
+    )
     grad_probs = jnp.einsum("bqhd,bkhd->bhqk", grad_h, value_h, preferred_element_type=jnp.float32)
     row_delta = jnp.einsum("bqhd,bqhd->bhq", grad_h, attended, preferred_element_type=jnp.float32)
     scores_bf = (softmax_w * (grad_probs - row_delta[:, :, :, None]) * score_scale).astype(
@@ -102,19 +124,13 @@
 
 
 def solution(mesh):
-    in_specs = (
-        P(("shard", "replica"), None),
-        P(("shard", "replica"), None),
-        P(("shard", "replica"), None),
-        P(("shard", "replica")),
-        P(("shard", "replica")),
-        P(None, "shard"),
-        P(("shard", "replica"), None),
+    shard_size, replica_size = mesh.devices.shape
+    split = Mesh(
+        np.asarray(mesh.devices).reshape(shard_size, replica_size // 2, 2),
+        ("shard", "rz", "core"),
     )
-    out_specs = (
-        P(("shard", "replica"), None),
-        P(("shard", "replica"), None),
-        P(("shard", "replica"), None),
-        P(None, "shard"),
-    )
-    return jax.shard_map(local, mesh=mesh, in_specs=in_specs, out_specs=out_specs, check_vma=False)
+    rows = P(("shard", "rz", "core"), None)
+    flat = P(("shard", "rz", "core"))
+    in_specs = (rows, rows, rows, flat, flat, P(None, "shard"), rows)
+    out_specs = (rows, rows, rows, P(None, "shard"))
+    return jax.shard_map(local, mesh=split, in_specs=in_specs, out_specs=out_specs, check_vma=False)

time: 303 us -> 212 us (0.70)
  waiting for transfers between devices: 103 us -> 51.8 us
  blocking collectives: 152 us -> 104 us
  starting transfers between devices: 13.5 us -> 19.8 us
  matrix products: 16.5 us -> 13.3 us
    all_to_all x2, waiting for transfers between devices: 103 us -> 51.8 us  [the longest x1 35.3 us: local(): lax.all_to_all(jnp.broadcast_to(weight_part[None], (shard_count,) + weigh...]
    all_to_all x2 -> x4, blocking collectives: 152 us -> 104 us  [the longest x1 53.8 us: local(): arrived = lax.all_to_all(pair_sum, 'shard', 0, 0, tiled=True)]
    all_to_all x2, starting transfers between devices: 13.5 us -> 19.8 us  [the longest x1 11.1 us: local(): lax.all_to_all(jnp.broadcast_to(piece_sum[None], (groups * cores,) + piec...]
    reduce_sum x0 -> x1, other arithmetic: none -> 3.23 us  [local(): pair_sum = jnp.sum(pair.astype(jnp.float32), axis=1).astype(jnp.bfloat16)]
    another operation x4 -> x3, local copies, waits for them, and re-layouts: 3.57 us -> 6.13 us
    unnamed x19 -> x21, local copies, waits for them, and re-layouts: 6.6 us -> 5.58 us
  transfers between devices with their start and end apart: 2 -> 2, of which waited for: 2 -> 2; matrix products, arithmetic and copies ran while one was open for 6% -> 10% of each run, Pallas kernels for 0% -> 0%
where the time goes in v2:
time: 212 us
  blocking collectives  104 us (49%)
  waiting for transfers between devices  51.8 us (24%)
  starting transfers between devices  19.8 us (9%)
  local copies, waits for them, and re-layouts  17.9 us (8%)
  matrix products  13.3 us (6%)
  other arithmetic  3.74 us (2%)
    all_to_all x1, blocking collectives, local(): arrived = lax.all_to_all(pair_sum, 'shard', 0, 0, tiled=True)  53.8 us
    all_to_all x1, waiting for transfers between devices, local(): lax.all_to_all(jnp.broadcast_to(weight_part[None], (shard_count,) + weigh...  35.3 us
    all_to_all x1, blocking collectives, local(): lax.all_to_all(padded.reshape(groups, piece_rows, -1), 'rz', 0, 0, tiled=...  29.9 us
    all_to_all x1, waiting for transfers between devices, local(): lax.all_to_all(jnp.broadcast_to(piece_sum[None], (groups * cores,) + piec...  16.6 us
    all_to_all x1, blocking collectives, local(): lax.all_to_all(jnp.broadcast_to(weight_blocks[None], (cores,) + weight_bl...  12.3 us
    all_to_all x1, starting transfers between devices, local(): lax.all_to_all(jnp.broadcast_to(piece_sum[None], (groups * cores,) + piec...  11.1 us
    all_to_all x1, starting transfers between devices, local(): lax.all_to_all(jnp.broadcast_to(weight_part[None], (shard_count,) + weigh...  8.68 us
    all_to_all x1, blocking collectives, local(): lax.all_to_all(term.reshape(shard_count, cores, part_rows, -1), 'core', 1...  8.17 us
  transfers between devices with their start and end apart: 2, of which 2 were waited for; matrix products, arithmetic and copies ran while one was open for 10% of the time, Pallas kernels for 0%

profile of v2, /device:TPU:1, one launch (start us, length us, event | category | flops | bytes accessed | tf_op | source)
XLA Modules:
  0.0 211.6 jit_solution(14789004159217420365)
XLA Ops:
  0.7 1.0 constant_dynamic-slice_fusion
  1.7 1.8 broadcast_in_dim.16
  3.4 8.7 %all-to-all-start = ((bf16[16,512,128]{2,1,0:T(8,128)(2,1)}), bf16[16,512,128]{2,1,0:T(8,128)(2,1)S(1)}, u32[]{:S(2)}, u32[]{:S(2)}) async-start(bf16[16,512,128]{2,1,0:T(8,128)(2,1)} %broadcast_in_dim.16), calls=%async_computation | async-start | bytes 4194304 | tf_op jit(solution)/shard_map/all_to_all | solution.py:26
  12.1 2.0 copy.121
  14.2 2.0 copy.123
  16.2 2.0 copy.122
  18.5 3.4 %fusion.18 = (f32[8,256]{1,0:T(8,128)S(1)}, f32[8,256,256]{1,2,0:T(8,128)}) fusion(pred[256,256]{0,1:T(8,128)(4,1)S(1)} %fusion.11, bf16[256,8,128]{0,2,1:T(8,128)(2,1)} %bitcast.83, bf16[256,8,128]{0,2,1:T(8,128)(2,1)} %bitcast.85), kind=kOutput, calls=%fused_computation.38 | convolution fusion | flops 136315136 | bytes 3219456 | tf_op jit(solution)/shard_map/sub | solution.py:67
  21.8 35.3 %all-to-all-done = bf16[16,512,128]{2,1,0:T(8,128)(2,1)S(1)} async-done(((bf16[16,512,128]{2,1,0:T(8,128)(2,1)}), bf16[16,512,128]{2,1,0:T(8,128)(2,1)S(1)}, u32[]{:S(2)}, u32[]{:S(2)}) %all-to-all-start) | async-done | bytes 2097184 | tf_op jit(solution)/shard_map/all_to_all | solution.py:26
  58.1 12.3 %all_to_all.30 = bf16[2,16,512,128]{3,2,1,0:T(8,128)(2,1)S(1)} all-to-all(bf16[2,16,512,128]{3,2,1,0:T(8,128)(2,1)S(1)} %broadcast_in_dim.17), channel_id=1, replica_groups=mesh['shard'=16,'rz'=24,'core'=2] {'core'}, dimensions={0} | all-to-all | bytes 8388608 | tf_op jit(solution)/shard_map/all_to_all | solution.py:33
  70.3 1.3 fusion.2
  72.4 1.3 multiply_convert_fusion
  74.2 8.2 %all_to_all.31 = bf16[16,2,512,128]{3,2,0,1:T(8,128)(2,1)} all-to-all(bf16[16,2,512,128]{3,2,0,1:T(8,128)(2,1)S(1)} %copy.100), channel_id=1, replica_groups=mesh['shard'=16,'rz'=24,'core'=2] {'core'}, dimensions={1} | all-to-all | bytes 8388608 | tf_op jit(solution)/shard_map/all_to_all | solution.py:84
  82.3 3.2 %reduce_sum.40 = bf16[16,512,128]{2,1,0:T(8,128)(2,1)S(1)} reduce(bf16[16,2,512,128]{3,2,0,1:T(8,128)(2,1)} %all_to_all.31, bf16[]{:T(256)} %constant.49.clone.1), dimensions={1}, to_apply=%region_2.3 | reduce | flops 1048576 | bytes 6291458 | tf_op jit(solution)/shard_map/reduce_sum | solution.py:87
  85.6 53.8 %all_to_all.32 = bf16[16,512,128]{2,1,0:T(8,128)(2,1)S(1)} all-to-all(bf16[16,512,128]{2,1,0:T(8,128)(2,1)S(1)} %reduce_sum.40), channel_id=1, replica_groups=mesh['shard'=16,'rz'=24,'core'=2] {'shard'}, dimensions={0} | all-to-all | bytes 4194304 | tf_op jit(solution)/shard_map/all_to_all | solution.py:88
  139.8 29.9 %all_to_all.33 = f32[24,22,128]{2,1,0:T(8,128)S(1)} all-to-all(f32[24,22,128]{2,1,0:T(8,128)S(1)} %reshape.309), channel_id=1, replica_groups=mesh['shard'=16,'rz'=24,'core'=2] {'rz'}, dimensions={0} | all-to-all | bytes 540672 | tf_op jit(solution)/shard_map/all_to_all | solution.py:93
  170.6 11.1 %all-to-all-start.5 = ((f32[48,22,128]{2,1,0:T(8,128)}), f32[48,22,128]{2,1,0:T(8,128)S(1)}, u32[]{:S(2)}, u32[]{:S(2)}) async-start(f32[48,22,128]{2,1,0:T(8,128)} %broadcast_in_dim.18), calls=%async_computation.5 | async-start | bytes 1179648 | tf_op jit(solution)/shard_map/all_to_all | solution.py:97
  181.8 2.4 %multiply_convert_fusion.1 = bf16[8,256,256]{1,2,0:T(8,128)(2,1)S(1)} fusion(bf16[256,8,128]{0,2,1:T(8,128)(2,1)S(1)} %bitcast.90, bf16[256,8,128]{0,2,1:T(8,128)(2,1)} %bitcast.94, f32[8,256]{1,0:T(8,128)S(1)} %get-tuple-element.28, f32[8,256,256]{1,2,0:T(8,128)} %get-tuple-element.27, f32[8,256]{1,0:T(8,128)S(1)} %get-tuple-element.26), kind=kOutput, calls=%fused_computation.3 | convolution fusion | flops 136839168 | bytes 4210688 | tf_op jit(solution)/shard_map/bqhd,bkhd->bhqk/dot_general | solution.py:110
  184.2 1.1 convolution_convert_fusion
  185.3 2.0 copy.104
  187.3 1.3 convolution_convert_fusion.3
  188.6 2.0 copy.105
  190.6 2.3 %convolution_convert_fusion.2 = bf16[8,128,256]{2,1,0:T(8,128)(2,1)S(1)} fusion(bf16[256,8,128]{0,2,1:T(8,128)(2,1)} %bitcast.95, f32[8,256,256]{1,2,0:T(8,128)} %get-tuple-element.27, f32[8,256]{1,0:T(8,128)S(1)} %get-tuple-element.26), kind=kOutput, calls=%fused_computation.10 | convolution fusion | flops 135528448 | bytes 3153920 | tf_op jit(solution)/shard_map/bhqk,bqhd->bkhd/dot_general | solution.py:117
  192.9 1.0 copy.106
  193.9 16.6 %all-to-all-done.5 = f32[48,22,128]{2,1,0:T(8,128)S(1)} async-done(((f32[48,22,128]{2,1,0:T(8,128)}), f32[48,22,128]{2,1,0:T(8,128)S(1)}, u32[]{:S(2)}, u32[]{:S(2)}) %all-to-all-start.5) | async-done | bytes 540704 | tf_op jit(solution)/shard_map/all_to_all | solution.py:97
  (33 shorter events, 4.8 us)
Async XLA Ops:
  0.6 69.7 %copy-start = (bf16[256,2048]{1,0:T(8,128)(2,1)S(1)}, bf16[256,2048]{1,0:T(8,128)(2,1)}, u32[]{:S(2)}) copy-start(bf16[256,2048]{1,0:T(8,128)(2,1)} %param.13) | copy-start | bytes 3145732
  3.4 53.7 %all-to-all-start = ((bf16[16,512,128]{2,1,0:T(8,128)(2,1)}), bf16[16,512,128]{2,1,0:T(8,128)(2,1)S(1)}, u32[]{:S(2)}, u32[]{:S(2)}) async-start(bf16[16,512,128]{2,1,0:T(8,128)(2,1)} %broadcast_in_dim.16), calls=%async_computation | async-start | bytes 4194304 | tf_op jit(solution)/shard_map/all_to_all | solution.py:26
  12.1 6.2 %copy-start.6 = (s32[256]{0:T(256)S(1)}, s32[256]{0:T(256)}, u32[]{:S(2)}) copy-start(s32[256]{0:T(256)} %param.11) | copy-start | bytes 3076
  12.1 6.2 %copy-start.5 = (s32[256]{0:T(256)S(1)}, s32[256]{0:T(256)}, u32[]{:S(2)}) copy-start(s32[256]{0:T(256)} %param.10) | copy-start | bytes 3076
  70.3 1.3 copy-start.3
  70.3 1.8 copy-start.8
  71.6 0.8 copy-start.7
  139.7 42.0 %copy-start.4 = (bf16[256,1024]{0,1:T(8,128)(2,1)S(1)}, bf16[256,1024]{0,1:T(8,128)(2,1)}, u32[]{:S(2)}) copy-start(bf16[256,1024]{0,1:T(8,128)(2,1)} %copy.123) | copy-start | bytes 1572868
  170.6 39.9 %all-to-all-start.5 = ((f32[48,22,128]{2,1,0:T(8,128)}), f32[48,22,128]{2,1,0:T(8,128)S(1)}, u32[]{:S(2)}, u32[]{:S(2)}) async-start(f32[48,22,128]{2,1,0:T(8,128)} %broadcast_in_dim.18), calls=%async_computation.5 | async-start | bytes 1179648 | tf_op jit(solution)/shard_map/all_to_all | solution.py:97
  181.8 2.4 %copy-start.2 = (bf16[256,1024]{0,1:T(8,128)(2,1)S(1)}, bf16[256,1024]{0,1:T(8,128)(2,1)}, u32[]{:S(2)}) copy-start(bf16[256,1024]{0,1:T(8,128)(2,1)} %copy.121) | copy-start | bytes 1572868
  184.1 3.2 %copy-start.1 = (bf16[256,1024]{0,1:T(8,128)(2,1)S(1)}, bf16[256,1024]{0,1:T(8,128)(2,1)}, u32[]{:S(2)}) copy-start(bf16[256,1024]{0,1:T(8,128)(2,1)} %copy.122) | copy-start | bytes 1572868

commit v3 on v2

--- a/solution.py
+++ b/solution.py
@@ -13,33 +13,81 @@
 SEQ = 256
 
 
+def rotate(blocks, shift, axis):
+    count = blocks.shape[axis]
+    doubled = jnp.concatenate([blocks, blocks], axis=axis)
+    return lax.dynamic_slice_in_dim(doubled, shift, count, axis=axis)
+
+
+def swap_in(block, x_at):
+    other = lax.ppermute(block, "xl", [(0, 1), (1, 0)])
+    return jnp.where(x_at == 0, jnp.stack([block, other]), jnp.stack([other, block]))
+
+
+def ring_gather(block, ys):
+    right = [(i, (i + 1) % ys) for i in range(ys)]
+    left = [(i, (i - 1) % ys) for i in range(ys)]
+    by_offset = {0: block}
+    moving = block
+    for d in range(1, ys // 2 + 1):
+        moving = lax.ppermute(moving, "y", right)
+        by_offset[(ys - d) % ys] = moving
+    moving = block
+    for d in range(1, (ys - 1) // 2 + 1):
+        moving = lax.ppermute(moving, "y", left)
+        by_offset[d] = moving
+    return jnp.stack([by_offset[o] for o in range(ys)])
+
+
+def ring_reduce(blocks, ys):
+    right = [(i, (i + 1) % ys) for i in range(ys)]
+    left = [(i, (i - 1) % ys) for i in range(ys)]
+    far_right = ys // 2
+    moving = blocks[far_right]
+    for d in range(far_right - 1, 0, -1):
+        moving = lax.ppermute(moving, "y", right)
+        moving = (moving.astype(jnp.float32) + blocks[d].astype(jnp.float32)).astype(blocks.dtype)
+    from_left = lax.ppermute(moving, "y", right)
+    far_left = far_right + 1
+    moving = blocks[far_left]
+    for d in range(far_left + 1, ys):
+        moving = lax.ppermute(moving, "y", left)
+        moving = (moving.astype(jnp.float32) + blocks[d].astype(jnp.float32)).astype(blocks.dtype)
+    from_right = lax.ppermute(moving, "y", left)
+    return (
+        blocks[0].astype(jnp.float32)
+        + from_left.astype(jnp.float32)
+        + from_right.astype(jnp.float32)
+    )
+
+
 def local(queries, keys, values, positions, live, out_weight, grad_out):
     tok_rows = queries.shape[0]
     seq_count = tok_rows // SEQ
     q_width = out_weight.shape[0]
     score_scale = 1.0 / math.sqrt(HEAD_DIM)
-    shard_count = lax.axis_size("shard")
+    ys = lax.axis_size("y")
+    xls = lax.axis_size("xl")
+    shard_count = ys * xls
     cores = lax.axis_size("core")
     core = lax.axis_index("core")
+    y_at = lax.axis_index("y")
+    x_at = lax.axis_index("xl")
     part_rows = q_width // cores
     weight_part = lax.dynamic_slice_in_dim(out_weight, core * part_rows, part_rows, axis=0)
-    weight_blocks = lax.all_to_all(
-        jnp.broadcast_to(weight_part[None], (shard_count,) + weight_part.shape),
-        "shard",
-        0,
-        0,
-        tiled=True,
-    )
+    weight_pair = swap_in(weight_part, x_at)
+    weight_ring = ring_gather(weight_pair, ys)
     weight_all = lax.all_to_all(
-        jnp.broadcast_to(weight_blocks[None], (cores,) + weight_blocks.shape),
+        jnp.broadcast_to(weight_ring[None], (cores,) + weight_ring.shape),
         "core",
         0,
         0,
         tiled=True,
     )
+    grad_rot = rotate(grad_out.reshape(tok_rows, ys, xls, -1), y_at, 1)
     grad_att32 = jnp.einsum(
-        "tjc,pjrc->tpr",
-        grad_out.reshape(tok_rows, shard_count, -1),
+        "toxc,poxrc->tpr",
+        grad_rot,
         weight_all,
         preferred_element_type=jnp.float32,
     ).reshape(tok_rows, q_width)
@@ -71,7 +119,7 @@
         "bhqk,bkhd->bqhd", probs_bf, value_h, preferred_element_type=jnp.float32
     ).astype(jnp.bfloat16)
     attended_rows = attended.reshape(tok_rows, q_width)
-    total_tokens = tok_rows * lax.axis_size("shard") * lax.axis_size("rz") * lax.axis_size("core")
+    total_tokens = tok_rows * lax.axis_size("y") * lax.axis_size("xl") * lax.axis_size("rz") * lax.axis_size("core")
     term = (
         jnp.einsum(
             "tr,tjc->jrc",
@@ -85,8 +133,11 @@
         term.reshape(shard_count, cores, part_rows, -1), "core", 1, 1, tiled=True
     )
     pair_sum = jnp.sum(pair.astype(jnp.float32), axis=1).astype(jnp.bfloat16)
-    arrived = lax.all_to_all(pair_sum, "shard", 0, 0, tiled=True)
-    shard_sum = jnp.sum(arrived.astype(jnp.float32), axis=0)
+    pair_rot = rotate(pair_sum.reshape(ys, xls, part_rows, -1), y_at, 0)
+    y_sum = ring_reduce(pair_rot, ys)
+    keep = jnp.where(x_at == 0, y_sum[0], y_sum[1])
+    send = jnp.where(x_at == 0, y_sum[1], y_sum[0])
+    shard_sum = keep + lax.ppermute(send, "xl", [(0, 1), (1, 0)])
     groups = lax.axis_size("rz")
     piece_rows = -(-part_rows // groups)
     padded = jnp.pad(shard_sum, ((0, piece_rows * groups - part_rows), (0, 0)))
@@ -126,11 +177,12 @@
 def solution(mesh):
     shard_size, replica_size = mesh.devices.shape
     split = Mesh(
-        np.asarray(mesh.devices).reshape(shard_size, replica_size // 2, 2),
-        ("shard", "rz", "core"),
+        np.asarray(mesh.devices).reshape(shard_size // 2, 2, replica_size // 2, 2),
+        ("y", "xl", "rz", "core"),
     )
-    rows = P(("shard", "rz", "core"), None)
-    flat = P(("shard", "rz", "core"))
-    in_specs = (rows, rows, rows, flat, flat, P(None, "shard"), rows)
-    out_specs = (rows, rows, rows, P(None, "shard"))
+    rows = P(("y", "xl", "rz", "core"), None)
+    flat = P(("y", "xl", "rz", "core"))
+    columns = P(None, ("y", "xl"))
+    in_specs = (rows, rows, rows, flat, flat, columns, rows)
+    out_specs = (rows, rows, rows, columns)
     return jax.shard_map(local, mesh=split, in_specs=in_specs, out_specs=out_specs, check_vma=False)

time: 212 us -> 211 us (level)
  blocking collectives: 104 us -> 46.4 us
  starting transfers between devices: 19.8 us -> 60.6 us
  waiting for transfers between devices: 51.8 us -> 65.6 us
  other arithmetic: 3.74 us -> 6.18 us
    all_to_all x2 -> x1, blocking collectives: 66.1 us -> 17.8 us  [local(): lax.all_to_all(jnp.broadcast_to(weight_ring[None], (cores,) + weight_ring...]
    ppermute x0 -> x16, starting transfers between devices: none -> 47.3 us  [the longest x3 14.7 us: ring_gather(): moving = lax.ppermute(moving, 'y', left)]
    ppermute x0 -> x16, waiting for transfers between devices: none -> 45.1 us  [the longest x3 18.7 us: ring_reduce(): moving = lax.ppermute(moving, 'y', right)]
    all_to_all x1 -> x0, waiting for transfers between devices: 35.3 us -> none  [local(): lax.all_to_all(jnp.broadcast_to(weight_part[None], (shard_count,) + weigh...]
    all_to_all x1, blocking collectives: 29.9 us -> 20.5 us  [local(): lax.all_to_all(padded.reshape(groups, piece_rows, -1), 'rz', 0, 0, tiled=...]
    all_to_all x1 -> x0, starting transfers between devices: 8.68 us -> none  [local(): lax.all_to_all(jnp.broadcast_to(weight_part[None], (shard_count,) + weigh...]
    all_to_all x1, waiting for transfers between devices: 16.6 us -> 20.5 us  [local(): lax.all_to_all(jnp.broadcast_to(piece_sum[None], (groups * cores,) + piec...]
    another operation x3 -> x6, local copies, waits for them, and re-layouts: 6.13 us -> 3.45 us
  transfers between devices with their start and end apart: 2 -> 17, of which waited for: 2 -> 11; matrix products, arithmetic and copies ran while one was open for 10% -> 9% of each run, Pallas kernels for 0% -> 0%
where the time goes in v3:
time: 211 us; the launch traced here: 210 us
  waiting for transfers between devices  65.6 us (31%)
  starting transfers between devices  60.6 us (29%)
  blocking collectives  46.4 us (22%)
  local copies, waits for them, and re-layouts  17.3 us (8%)
  matrix products  12.8 us (6%)
  other arithmetic  6.18 us (3%)
    all_to_all x1, blocking collectives, local(): lax.all_to_all(padded.reshape(groups, piece_rows, -1), 'rz', 0, 0, tiled=...  20.5 us
    all_to_all x1, waiting for transfers between devices, local(): lax.all_to_all(jnp.broadcast_to(piece_sum[None], (groups * cores,) + piec...  20.5 us
    ppermute x3, waiting for transfers between devices, ring_reduce(): moving = lax.ppermute(moving, 'y', right)  18.7 us
    all_to_all x1, blocking collectives, local(): lax.all_to_all(jnp.broadcast_to(weight_ring[None], (cores,) + weight_ring...  17.8 us
    ppermute x3, starting transfers between devices, ring_gather(): moving = lax.ppermute(moving, 'y', left)  14.7 us
    ppermute x4, waiting for transfers between devices, ring_gather(): moving = lax.ppermute(moving, 'y', right)  13.7 us
    all_to_all x1, starting transfers between devices, local(): lax.all_to_all(jnp.broadcast_to(piece_sum[None], (groups * cores,) + piec...  13.3 us
    all_to_all x1, blocking collectives, local(): lax.all_to_all(term.reshape(shard_count, cores, part_rows, -1), 'core', 1...  8.16 us
  transfers between devices with their start and end apart: 17, of which 11 were waited for; matrix products, arithmetic and copies ran while one was open for 9% of the time, Pallas kernels for 0%

profile of v3, /device:TPU:1, one launch (start us, length us, event | category | flops | bytes accessed | tf_op | source)
XLA Modules:
  0.0 210.1 jit_solution(13941424563232166565)
XLA Ops:
  1.6 3.9 %collective-permute-start = (bf16[512,128]{1,0:T(8,128)(2,1)S(1)}, bf16[512,128]{1,0:T(8,128)(2,1)S(1)}, u32[]{:S(2)}, u32[]{:S(2)}) collective-permute-start(bf16[512,128]{1,0:T(8,128)(2,1)S(1)} %constant_dynamic-slice_fusion), channel_id=1, source_target_pairs={{0,48},{48,0},{1,49},{49,1},{2,50},{50,2},{3,51},{51,3},{4,52},{52... | collective-permute-start | bytes 393224 | tf_op jit(solution)/shard_map/ppermute | solution.py:23
  7.9 5.9 %collective-permute-start.1 = (bf16[2,512,128]{2,1,0:T(8,128)(2,1)S(1)}, bf16[2,512,128]{2,1,0:T(8,128)(2,1)}, u32[]{:S(2)}, u32[]{:S(2)}) collective-permute-start(bf16[2,512,128]{2,1,0:T(8,128)(2,1)S(1)} %maximum_select_fusion.1), channel_id=1, source_target_pairs={{0,672},{96,0},{192,96},{288,192},{384,288},{480,384},{576,480},{6... | collective-permute-start | bytes 786440 | tf_op jit(solution)/shard_map/ppermute | solution.py:37
  18.1 4.6 %collective-permute-start.2 = (bf16[2,512,128]{2,1,0:T(8,128)(2,1)}, bf16[2,512,128]{2,1,0:T(8,128)(2,1)}, u32[]{:S(2)}, u32[]{:S(2)}) collective-permute-start(bf16[2,512,128]{2,1,0:T(8,128)(2,1)} %collective-permute-done.1), channel_id=1, source_target_pairs={{0,672},{96,0},{192,96},{288,192},{384,288},{480,384},{576,480},{6... | collective-permute-start | bytes 786440 | tf_op jit(solution)/shard_map/ppermute | solution.py:37
  24.6 2.2 %fusion.30 = (f32[8,256]{1,0:T(8,128)S(1)}, f32[8,256,256]{1,2,0:T(8,128)}) fusion(pred[256,256]{0,1:T(8,128)(4,1)S(1)} %fusion.21, bf16[256,8,128]{0,2,1:T(8,128)(2,1)S(1)} %bitcast.145, bf16[256,8,128]{0,2,1:T(8,128)(2,1)S(1)} %bitcast.147), kind=kOutput, calls=%fused_computation.76 | convolution fusion | flops 136315136 | bytes 3219456 | tf_op jit(solution)/shard_map/sub | solution.py:115
  29.7 2.9 %collective-permute-done.5 = bf16[2,512,128]{2,1,0:T(8,128)(2,1)} collective-permute-done((bf16[2,512,128]{2,1,0:T(8,128)(2,1)}, bf16[2,512,128]{2,1,0:T(8,128)(2,1)}, u32[]{:S(2)}, u32[]{:S(2)}) %collective-permute-start.5) | collective-permute-done | bytes 262176 | tf_op jit(solution)/shard_map/ppermute | solution.py:33
  32.6 2.3 %collective-permute-start.6 = (bf16[2,512,128]{2,1,0:T(8,128)(2,1)}, bf16[2,512,128]{2,1,0:T(8,128)(2,1)S(1)}, u32[]{:S(2)}, u32[]{:S(2)}) collective-permute-start(bf16[2,512,128]{2,1,0:T(8,128)(2,1)} %collective-permute-done.5), channel_id=1, source_target_pairs={{0,96},{96,192},{192,288},{288,384},{384,480},{480,576},{576,672},... | collective-permute-start | bytes 786440 | tf_op jit(solution)/shard_map/ppermute | solution.py:33
  35.0 4.2 %collective-permute-start.3 = (bf16[2,512,128]{2,1,0:T(8,128)(2,1)}, bf16[2,512,128]{2,1,0:T(8,128)(2,1)S(1)}, u32[]{:S(2)}, u32[]{:S(2)}) collective-permute-start(bf16[2,512,128]{2,1,0:T(8,128)(2,1)} %collective-permute-done.2), channel_id=1, source_target_pairs={{0,672},{96,0},{192,96},{288,192},{384,288},{480,384},{576,480},{6... | collective-permute-start | bytes 786440 | tf_op jit(solution)/shard_map/ppermute | solution.py:37
  40.2 3.4 %collective-permute-done.6 = bf16[2,512,128]{2,1,0:T(8,128)(2,1)S(1)} collective-permute-done((bf16[2,512,128]{2,1,0:T(8,128)(2,1)}, bf16[2,512,128]{2,1,0:T(8,128)(2,1)S(1)}, u32[]{:S(2)}, u32[]{:S(2)}) %collective-permute-start.6) | collective-permute-done | bytes 262176 | tf_op jit(solution)/shard_map/ppermute | solution.py:33
  46.6 7.4 %collective-permute-done.7 = bf16[2,512,128]{2,1,0:T(8,128)(2,1)S(1)} collective-permute-done((bf16[2,512,128]{2,1,0:T(8,128)(2,1)S(1)}, bf16[2,512,128]{2,1,0:T(8,128)(2,1)S(1)}, u32[]{:S(2)}, u32[]{:S(2)}) %collective-permute-start.7) | collective-permute-done | bytes 262176 | tf_op jit(solution)/shard_map/ppermute | solution.py:33
  57.2 17.8 %all_to_all.20 = bf16[2,8,2,512,128]{4,3,2,1,0:T(8,128)(2,1)S(1)} all-to-all(bf16[2,8,2,512,128]{4,3,2,1,0:T(8,128)(2,1)S(1)} %broadcast_in_dim.14), channel_id=1, replica_groups=mesh['y'=8,'xl'=2,'rz'=24,'core'=2] {'core'}, dimensions={0} | all-to-all | bytes 8388608 | tf_op jit(solution)/shard_map/all_to_all | solution.py:80
  82.2 8.2 %all_to_all.21 = bf16[16,2,512,128]{3,2,0,1:T(8,128)(2,1)} all-to-all(bf16[16,2,512,128]{3,2,0,1:T(8,128)(2,1)S(1)} %copy.88), channel_id=1, replica_groups=mesh['y'=8,'xl'=2,'rz'=24,'core'=2] {'core'}, dimensions={1} | all-to-all | bytes 8388608 | tf_op jit(solution)/shard_map/all_to_all | solution.py:132
  90.4 3.2 %reduce_sum.31 = bf16[16,512,128]{2,1,0:T(8,128)(2,1)S(1)} reduce(bf16[16,2,512,128]{3,2,0,1:T(8,128)(2,1)} %all_to_all.21, bf16[]{:T(256)} %constant.59.clone.1), dimensions={1}, to_apply=%region_2.3 | reduce | flops 1048576 | bytes 6291458 | tf_op jit(solution)/shard_map/reduce_sum | solution.py:135
  96.4 8.7 %collective-permute-done.8 = bf16[2,512,128]{2,1,0:T(8,128)(2,1)S(1)} collective-permute-done((bf16[2,512,128]{2,1,0:T(8,128)(2,1)S(1)}, bf16[2,512,128]{2,1,0:T(8,128)(2,1)S(1)}, u32[]{:S(2)}, u32[]{:S(2)}) %collective-permute-start.8) | collective-permute-done | bytes 262176 | tf_op jit(solution)/shard_map/ppermute | solution.py:48
  107.1 4.6 %collective-permute-start.12 = (bf16[2,512,128]{2,1,0:T(8,128)(2,1)S(1)}, bf16[2,512,128]{2,1,0:T(8,128)(2,1)S(1)}, u32[]{:S(2)}, u32[]{:S(2)}) collective-permute-start(bf16[2,512,128]{2,1,0:T(8,128)(2,1)S(1)} %get-tuple-element.23), channel_id=1, source_target_pairs={{0,672},{96,0},{192,96},{288,192},{384,288},{480,384},{576,480},{6... | collective-permute-start | bytes 786440 | tf_op jit(solution)/shard_map/ppermute | solution.py:54
  111.7 3.2 %collective-permute-done.9 = bf16[2,512,128]{2,1,0:T(8,128)(2,1)S(1)} collective-permute-done((bf16[2,512,128]{2,1,0:T(8,128)(2,1)S(1)}, bf16[2,512,128]{2,1,0:T(8,128)(2,1)S(1)}, u32[]{:S(2)}, u32[]{:S(2)}) %collective-permute-start.9) | collective-permute-done | bytes 262176 | tf_op jit(solution)/shard_map/ppermute | solution.py:48
  116.9 6.8 %collective-permute-done.10 = bf16[2,512,128]{2,1,0:T(8,128)(2,1)S(1)} collective-permute-done((bf16[2,512,128]{2,1,0:T(8,128)(2,1)S(1)}, bf16[2,512,128]{2,1,0:T(8,128)(2,1)S(1)}, u32[]{:S(2)}, u32[]{:S(2)}) %collective-permute-start.10) | collective-permute-done | bytes 262176 | tf_op jit(solution)/shard_map/ppermute | solution.py:48
  125.8 3.4 %collective-permute-start.11 = (bf16[2,512,128]{2,1,0:T(8,128)(2,1)S(1)}, bf16[2,512,128]{2,1,0:T(8,128)(2,1)S(1)}, u32[]{:S(2)}, u32[]{:S(2)}) collective-permute-start(bf16[2,512,128]{2,1,0:T(8,128)(2,1)S(1)} %get-tuple-element.20), channel_id=1, source_target_pairs={{0,96},{96,192},{192,288},{288,384},{384,480},{480,576},{576,672},... | collective-permute-start | bytes 786440 | tf_op jit(solution)/shard_map/ppermute | solution.py:50
  131.1 3.1 %collective-permute-start.14 = (bf16[2,512,128]{2,1,0:T(8,128)(2,1)S(1)}, bf16[2,512,128]{2,1,0:T(8,128)(2,1)S(1)}, u32[]{:S(2)}, u32[]{:S(2)}) collective-permute-start(bf16[2,512,128]{2,1,0:T(8,128)(2,1)S(1)} %fusion.14), channel_id=1, source_target_pairs={{0,672},{96,0},{192,96},{288,192},{384,288},{480,384},{576,480},{6... | collective-permute-start | bytes 786440 | tf_op jit(solution)/shard_map/ppermute | solution.py:56
  134.2 4.0 %collective-permute-done.14 = bf16[2,512,128]{2,1,0:T(8,128)(2,1)S(1)} collective-permute-done((bf16[2,512,128]{2,1,0:T(8,128)(2,1)S(1)}, bf16[2,512,128]{2,1,0:T(8,128)(2,1)S(1)}, u32[]{:S(2)}, u32[]{:S(2)}) %collective-permute-start.14) | collective-permute-done | bytes 262176 | tf_op jit(solution)/shard_map/ppermute | solution.py:56
  140.2 5.2 %collective-permute-done.15 = f32[512,128]{1,0:T(8,128)S(1)} collective-permute-done((f32[512,128]{1,0:T(8,128)S(1)}, f32[512,128]{1,0:T(8,128)S(1)}, u32[]{:S(2)}, u32[]{:S(2)}) %collective-permute-start.15) | collective-permute-done | bytes 262176 | tf_op jit(solution)/shard_map/ppermute | solution.py:140
  145.6 20.5 %all_to_all.22 = f32[24,22,128]{2,1,0:T(8,128)S(1)} all-to-all(f32[24,22,128]{2,1,0:T(8,128)S(1)} %reshape.390), channel_id=1, replica_groups=mesh['y'=8,'xl'=2,'rz'=24,'core'=2] {'rz'}, dimensions={0} | all-to-all | bytes 540672 | tf_op jit(solution)/shard_map/all_to_all | solution.py:144
  166.9 13.3 %all-to-all-start.3 = ((f32[48,22,128]{2,1,0:T(8,128)}), f32[48,22,128]{2,1,0:T(8,128)S(1)}, u32[]{:S(2)}, u32[]{:S(2)}) async-start(f32[48,22,128]{2,1,0:T(8,128)} %broadcast_in_dim.15), calls=%async_computation.3 | async-start | bytes 1179648 | tf_op jit(solution)/shard_map/all_to_all | solution.py:148
  180.3 2.3 %multiply_convert_fusion.1 = bf16[8,256,256]{1,2,0:T(8,128)(2,1)S(1)} fusion(bf16[256,8,128]{0,2,1:T(8,128)(2,1)S(1)} %bitcast.154, bf16[256,8,128]{0,2,1:T(8,128)(2,1)} %bitcast.156, f32[8,256]{1,0:T(8,128)S(1)} %get-tuple-element.28, f32[8,256,256]{1,2,0:T(8,128)} %get-tuple-element.27, f32[8,256]{1,0:T(8,128)S(1)} %get-tuple-element.26), kind=kOutput, calls=%fused_computation.7 | convolution fusion | flops 136839168 | bytes 4210688 | tf_op jit(solution)/shard_map/bqhd,bkhd->bhqk/dot_general | solution.py:161
  188.5 20.5 %all-to-all-done.3 = f32[48,22,128]{2,1,0:T(8,128)S(1)} async-done(((f32[48,22,128]{2,1,0:T(8,128)}), f32[48,22,128]{2,1,0:T(8,128)S(1)}, u32[]{:S(2)}, u32[]{:S(2)}) %all-to-all-start.3) | async-done | bytes 540704 | tf_op jit(solution)/shard_map/all_to_all | solution.py:148
  (83 shorter events, 47.4 us)
Async XLA Ops:
  0.6 17.0 %copy-start.3 = (bf16[256,1024]{1,0:T(8,128)(2,1)S(1)}, bf16[256,1024]{1,0:T(8,128)(2,1)}, u32[]{:S(2)}) copy-start(bf16[256,1024]{1,0:T(8,128)(2,1)} %param.7) | copy-start | bytes 1572868
  1.6 6.3 %collective-permute-start = (bf16[512,128]{1,0:T(8,128)(2,1)S(1)}, bf16[512,128]{1,0:T(8,128)(2,1)S(1)}, u32[]{:S(2)}, u32[]{:S(2)}) collective-permute-start(bf16[512,128]{1,0:T(8,128)(2,1)S(1)} %constant_dynamic-slice_fusion), channel_id=1, source_target_pairs={{0,48},{48,0},{1,49},{49,1},{2,50},{50,2},{3,51},{51,3},{4,52},{52... | collective-permute-start | bytes 393224 | tf_op jit(solution)/shard_map/ppermute | solution.py:23
  7.9 10.2 %collective-permute-start.1 = (bf16[2,512,128]{2,1,0:T(8,128)(2,1)S(1)}, bf16[2,512,128]{2,1,0:T(8,128)(2,1)}, u32[]{:S(2)}, u32[]{:S(2)}) collective-permute-start(bf16[2,512,128]{2,1,0:T(8,128)(2,1)S(1)} %maximum_select_fusion.1), channel_id=1, source_target_pairs={{0,672},{96,0},{192,96},{288,192},{384,288},{480,384},{576,480},{6... | collective-permute-start | bytes 786440 | tf_op jit(solution)/shard_map/ppermute | solution.py:37
  13.8 8.9 %collective-permute-start.4 = (bf16[2,512,128]{2,1,0:T(8,128)(2,1)S(1)}, bf16[2,512,128]{2,1,0:T(8,128)(2,1)}, u32[]{:S(2)}, u32[]{:S(2)}) collective-permute-start(bf16[2,512,128]{2,1,0:T(8,128)(2,1)S(1)} %maximum_select_fusion.1), channel_id=1, source_target_pairs={{0,96},{96,192},{192,288},{288,384},{384,480},{480,576},{576,672},... | collective-permute-start | bytes 786440 | tf_op jit(solution)/shard_map/ppermute | solution.py:33
  18.1 16.9 %collective-permute-start.2 = (bf16[2,512,128]{2,1,0:T(8,128)(2,1)}, bf16[2,512,128]{2,1,0:T(8,128)(2,1)}, u32[]{:S(2)}, u32[]{:S(2)}) collective-permute-start(bf16[2,512,128]{2,1,0:T(8,128)(2,1)} %collective-permute-done.1), channel_id=1, source_target_pairs={{0,672},{96,0},{192,96},{288,192},{384,288},{480,384},{576,480},{6... | collective-permute-start | bytes 786440 | tf_op jit(solution)/shard_map/ppermute | solution.py:37
  22.7 10.0 %collective-permute-start.5 = (bf16[2,512,128]{2,1,0:T(8,128)(2,1)}, bf16[2,512,128]{2,1,0:T(8,128)(2,1)}, u32[]{:S(2)}, u32[]{:S(2)}) collective-permute-start(bf16[2,512,128]{2,1,0:T(8,128)(2,1)} %collective-permute-done.4), channel_id=1, source_target_pairs={{0,96},{96,192},{192,288},{288,384},{384,480},{480,576},{576,672},... | collective-permute-start | bytes 786440 | tf_op jit(solution)/shard_map/ppermute | solution.py:33
  24.6 2.2 %copy-start.4 = (bf16[256,1024]{1,0:T(8,128)(2,1)S(1)}, bf16[256,1024]{1,0:T(8,128)(2,1)}, u32[]{:S(2)}) copy-start(bf16[256,1024]{1,0:T(8,128)(2,1)} %param.9) | copy-start | bytes 1572868
  24.6 3.2 %copy-start.1 = (bf16[256,2048]{1,0:T(8,128)(2,1)S(1)}, bf16[256,2048]{1,0:T(8,128)(2,1)}, u32[]{:S(2)}) copy-start(bf16[256,2048]{1,0:T(8,128)(2,1)} %param.13) | copy-start | bytes 3145732
  32.6 11.0 %collective-permute-start.6 = (bf16[2,512,128]{2,1,0:T(8,128)(2,1)}, bf16[2,512,128]{2,1,0:T(8,128)(2,1)S(1)}, u32[]{:S(2)}, u32[]{:S(2)}) collective-permute-start(bf16[2,512,128]{2,1,0:T(8,128)(2,1)} %collective-permute-done.5), channel_id=1, source_target_pairs={{0,96},{96,192},{192,288},{288,384},{384,480},{480,576},{576,672},... | collective-permute-start | bytes 786440 | tf_op jit(solution)/shard_map/ppermute | solution.py:33
  35.0 11.5 %collective-permute-start.3 = (bf16[2,512,128]{2,1,0:T(8,128)(2,1)}, bf16[2,512,128]{2,1,0:T(8,128)(2,1)S(1)}, u32[]{:S(2)}, u32[]{:S(2)}) collective-permute-start(bf16[2,512,128]{2,1,0:T(8,128)(2,1)} %collective-permute-done.2), channel_id=1, source_target_pairs={{0,672},{96,0},{192,96},{288,192},{384,288},{480,384},{576,480},{6... | collective-permute-start | bytes 786440 | tf_op jit(solution)/shard_map/ppermute | solution.py:37
  43.6 10.3 %collective-permute-start.7 = (bf16[2,512,128]{2,1,0:T(8,128)(2,1)S(1)}, bf16[2,512,128]{2,1,0:T(8,128)(2,1)S(1)}, u32[]{:S(2)}, u32[]{:S(2)}) collective-permute-start(bf16[2,512,128]{2,1,0:T(8,128)(2,1)S(1)} %collective-permute-done.6), channel_id=1, source_target_pairs={{0,96},{96,192},{192,288},{288,384},{384,480},{480,576},{576,672},... | collective-permute-start | bytes 786440 | tf_op jit(solution)/shard_map/ppermute | solution.py:33
  57.2 17.8 %copy-start.2 = (bf16[256,8,2,128]{3,0,2,1:T(8,128)(2,1)S(1)}, bf16[256,8,2,128]{3,0,2,1:T(8,128)(2,1)}, u32[]{:S(2)}) copy-start(bf16[256,8,2,128]{3,0,2,1:T(8,128)(2,1)} %copy.73) | copy-start | bytes 3145732
  75.0 3.3 %copy-start.5 = (bf16[256,1024]{0,1:T(8,128)(2,1)S(1)}, bf16[256,1024]{0,1:T(8,128)(2,1)}, u32[]{:S(2)}) copy-start(bf16[256,1024]{0,1:T(8,128)(2,1)} %copy.112) | copy-start | bytes 1572868
  78.4 2.1 %copy-start.7 = (bf16[256,2,512]{0,2,1:T(8,128)(2,1)}, bf16[256,2,512]{0,2,1:T(8,128)(2,1)S(1)}, u32[]{:S(2)}) copy-start(bf16[256,2,512]{0,2,1:T(8,128)(2,1)S(1)} %copy.76) | copy-start | bytes 1572868
  94.5 10.6 %collective-permute-start.8 = (bf16[2,512,128]{2,1,0:T(8,128)(2,1)S(1)}, bf16[2,512,128]{2,1,0:T(8,128)(2,1)S(1)}, u32[]{:S(2)}, u32[]{:S(2)}) collective-permute-start(bf16[2,512,128]{2,1,0:T(8,128)(2,1)S(1)} %get-tuple-element.22), channel_id=1, source_target_pairs={{0,96},{96,192},{192,288},{288,384},{384,480},{480,576},{576,672},... | collective-permute-start | bytes 786440 | tf_op jit(solution)/shard_map/ppermute | solution.py:48
  105.2 9.7 %collective-permute-start.9 = (bf16[2,512,128]{2,1,0:T(8,128)(2,1)S(1)}, bf16[2,512,128]{2,1,0:T(8,128)(2,1)S(1)}, u32[]{:S(2)}, u32[]{:S(2)}) collective-permute-start(bf16[2,512,128]{2,1,0:T(8,128)(2,1)S(1)} %fusion.18), channel_id=1, source_target_pairs={{0,96},{96,192},{192,288},{288,384},{384,480},{480,576},{576,672},... | collective-permute-start | bytes 786440 | tf_op jit(solution)/shard_map/ppermute | solution.py:48
  107.1 9.8 %collective-permute-start.12 = (bf16[2,512,128]{2,1,0:T(8,128)(2,1)S(1)}, bf16[2,512,128]{2,1,0:T(8,128)(2,1)S(1)}, u32[]{:S(2)}, u32[]{:S(2)}) collective-permute-start(bf16[2,512,128]{2,1,0:T(8,128)(2,1)S(1)} %get-tuple-element.23), channel_id=1, source_target_pairs={{0,672},{96,0},{192,96},{288,192},{384,288},{480,384},{576,480},{6... | collective-permute-start | bytes 786440 | tf_op jit(solution)/shard_map/ppermute | solution.py:54
  114.9 8.8 %collective-permute-start.10 = (bf16[2,512,128]{2,1,0:T(8,128)(2,1)S(1)}, bf16[2,512,128]{2,1,0:T(8,128)(2,1)S(1)}, u32[]{:S(2)}, u32[]{:S(2)}) collective-permute-start(bf16[2,512,128]{2,1,0:T(8,128)(2,1)S(1)} %fusion.17), channel_id=1, source_target_pairs={{0,96},{96,192},{192,288},{288,384},{384,480},{480,576},{576,672},... | collective-permute-start | bytes 786440 | tf_op jit(solution)/shard_map/ppermute | solution.py:48
  123.9 7.1 %collective-permute-start.13 = (bf16[2,512,128]{2,1,0:T(8,128)(2,1)S(1)}, bf16[2,512,128]{2,1,0:T(8,128)(2,1)S(1)}, u32[]{:S(2)}, u32[]{:S(2)}) collective-permute-start(bf16[2,512,128]{2,1,0:T(8,128)(2,1)S(1)} %get-tuple-element.21), channel_id=1, source_target_pairs={{0,672},{96,0},{192,96},{288,192},{384,288},{480,384},{576,480},{6... | collective-permute-start | bytes 786440 | tf_op jit(solution)/shard_map/ppermute | solution.py:54
  125.8 8.4 %collective-permute-start.11 = (bf16[2,512,128]{2,1,0:T(8,128)(2,1)S(1)}, bf16[2,512,128]{2,1,0:T(8,128)(2,1)S(1)}, u32[]{:S(2)}, u32[]{:S(2)}) collective-permute-start(bf16[2,512,128]{2,1,0:T(8,128)(2,1)S(1)} %get-tuple-element.20), channel_id=1, source_target_pairs={{0,96},{96,192},{192,288},{288,384},{384,480},{480,576},{576,672},... | collective-permute-start | bytes 786440 | tf_op jit(solution)/shard_map/ppermute | solution.py:50
  131.1 7.1 %collective-permute-start.14 = (bf16[2,512,128]{2,1,0:T(8,128)(2,1)S(1)}, bf16[2,512,128]{2,1,0:T(8,128)(2,1)S(1)}, u32[]{:S(2)}, u32[]{:S(2)}) collective-permute-start(bf16[2,512,128]{2,1,0:T(8,128)(2,1)S(1)} %fusion.14), channel_id=1, source_target_pairs={{0,672},{96,0},{192,96},{288,192},{384,288},{480,384},{576,480},{6... | collective-permute-start | bytes 786440 | tf_op jit(solution)/shard_map/ppermute | solution.py:56
  138.3 7.1 %collective-permute-start.15 = (f32[512,128]{1,0:T(8,128)S(1)}, f32[512,128]{1,0:T(8,128)S(1)}, u32[]{:S(2)}, u32[]{:S(2)}) collective-permute-start(f32[512,128]{1,0:T(8,128)S(1)} %select_bitcast_fusion), channel_id=1, source_target_pairs={{0,48},{48,0},{1,49},{49,1},{2,50},{50,2},{3,51},{51,3},{4,52},{52... | collective-permute-start | bytes 786440 | tf_op jit(solution)/shard_map/ppermute | solution.py:140
  145.5 34.8 %copy-start.6 = (bf16[256,1024]{0,1:T(8,128)(2,1)S(1)}, bf16[256,1024]{0,1:T(8,128)(2,1)}, u32[]{:S(2)}) copy-start(bf16[256,1024]{0,1:T(8,128)(2,1)} %copy.112) | copy-start | bytes 1572868
  166.9 42.0 %all-to-all-start.3 = ((f32[48,22,128]{2,1,0:T(8,128)}), f32[48,22,128]{2,1,0:T(8,128)S(1)}, u32[]{:S(2)}, u32[]{:S(2)}) async-start(f32[48,22,128]{2,1,0:T(8,128)} %broadcast_in_dim.15), calls=%async_computation.3 | async-start | bytes 1179648 | tf_op jit(solution)/shard_map/all_to_all | solution.py:148
  (2 other events, 2.4 us)

commit v4 on v3

--- a/solution.py
+++ b/solution.py
@@ -76,26 +76,9 @@
     part_rows = q_width // cores
     weight_part = lax.dynamic_slice_in_dim(out_weight, core * part_rows, part_rows, axis=0)
     weight_pair = swap_in(weight_part, x_at)
-    weight_ring = ring_gather(weight_pair, ys)
-    weight_all = lax.all_to_all(
-        jnp.broadcast_to(weight_ring[None], (cores,) + weight_ring.shape),
-        "core",
-        0,
-        0,
-        tiled=True,
-    )
-    grad_rot = rotate(grad_out.reshape(tok_rows, ys, xls, -1), y_at, 1)
-    grad_att32 = jnp.einsum(
-        "toxc,poxrc->tpr",
-        grad_rot,
-        weight_all,
-        preferred_element_type=jnp.float32,
-    ).reshape(tok_rows, q_width)
-    grad_att = grad_att32.astype(jnp.bfloat16)
     query_h = queries.reshape(seq_count, SEQ, HEADS, HEAD_DIM)
     key_h = keys.reshape(seq_count, SEQ, HEADS, HEAD_DIM)
     value_h = values.reshape(seq_count, SEQ, HEADS, HEAD_DIM)
-    grad_h = grad_att.reshape(seq_count, SEQ, HEADS, HEAD_DIM)
     grid_index = positions.reshape(seq_count, SEQ)
     alive = live.reshape(seq_count, SEQ)
     frames_of = grid_index // PATCHES
@@ -134,6 +117,24 @@
     )
     pair_sum = jnp.sum(pair.astype(jnp.float32), axis=1).astype(jnp.bfloat16)
     pair_rot = rotate(pair_sum.reshape(ys, xls, part_rows, -1), y_at, 0)
+    weight_pair, pair_rot = lax.optimization_barrier((weight_pair, pair_rot))
+    weight_ring = ring_gather(weight_pair, ys)
+    weight_all = lax.all_to_all(
+        jnp.broadcast_to(weight_ring[None], (cores,) + weight_ring.shape),
+        "core",
+        0,
+        0,
+        tiled=True,
+    )
+    grad_rot = rotate(grad_out.reshape(tok_rows, ys, xls, -1), y_at, 1)
+    grad_att32 = jnp.einsum(
+        "toxc,poxrc->tpr",
+        grad_rot,
+        weight_all,
+        preferred_element_type=jnp.float32,
+    ).reshape(tok_rows, q_width)
+    grad_att = grad_att32.astype(jnp.bfloat16)
+    grad_h = grad_att.reshape(seq_count, SEQ, HEADS, HEAD_DIM)
     y_sum = ring_reduce(pair_rot, ys)
     keep = jnp.where(x_at == 0, y_sum[0], y_sum[1])
     send = jnp.where(x_at == 0, y_sum[1], y_sum[0])

time: 211 us -> 188 us (0.89)
  blocking collectives: 46.4 us -> 0 us
  starting transfers between devices: 60.6 us -> 91.3 us
  waiting for transfers between devices: 65.6 us -> 38.1 us
  local copies, waits for them, and re-layouts: 17.3 us -> 28.4 us
  other arithmetic: 6.18 us -> 11.5 us
  matrix products: 12.8 us -> 16 us
    all_to_all x3 -> x0, blocking collectives: 46.4 us -> none  [the longest x1 20.5 us: local(): lax.all_to_all(padded.reshape(groups, piece_rows, -1), 'rz', 0, 0, tiled=...]
    all_to_all x0 -> x3, starting transfers between devices: none -> 37 us  [the longest x1 14.1 us: local(): lax.all_to_all(term.reshape(shard_count, cores, part_rows, -1), 'core', 1...]
    all_to_all x0 -> x3, waiting for transfers between devices: none -> 18.3 us  [the longest x1 10 us: local(): lax.all_to_all(padded.reshape(groups, piece_rows, -1), 'rz', 0, 0, tiled=...]
    ppermute x3, waiting for transfers between devices: 18.7 us -> 5.37 us  [ring_reduce(): moving = lax.ppermute(moving, 'y', right)]
    ppermute x4, waiting for transfers between devices: 13.7 us -> 1.3 us  [ring_gather(): moving = lax.ppermute(moving, 'y', right)]
    all_to_all x1, waiting for transfers between devices: 20.5 us -> 12.7 us  [local(): lax.all_to_all(jnp.broadcast_to(piece_sum[None], (groups * cores,) + piec...]
    all_to_all x1, starting transfers between devices: 13.3 us -> 6 us  [local(): lax.all_to_all(jnp.broadcast_to(piece_sum[None], (groups * cores,) + piec...]
    ppermute x3, starting transfers between devices: 14.7 us -> 8.8 us  [ring_gather(): moving = lax.ppermute(moving, 'y', left)]
  transfers between devices with their start and end apart: 17 -> 20, of which waited for: 11 -> 8; matrix products, arithmetic and copies ran while one was open for 9% -> 25% of each run, Pallas kernels for 0% -> 0%
where the time goes in v4:
time: 188 us; the launch traced here: 186 us
  starting transfers between devices  91.3 us (49%)
  waiting for transfers between devices  38.1 us (20%)
  local copies, waits for them, and re-layouts  28.4 us (15%)
  matrix products  16 us (9%)
  other arithmetic  11.5 us (6%)
    all_to_all x1, starting transfers between devices, local(): lax.all_to_all(term.reshape(shard_count, cores, part_rows, -1), 'core', 1...  14.1 us
    all_to_all x1, waiting for transfers between devices, local(): lax.all_to_all(jnp.broadcast_to(piece_sum[None], (groups * cores,) + piec...  12.7 us
    all_to_all x1, starting transfers between devices, local(): lax.all_to_all(jnp.broadcast_to(weight_ring[None], (cores,) + weight_ring...  12 us
    unnamed x31, local copies, waits for them, and re-layouts  11.6 us
    all_to_all x1, starting transfers between devices, local(): lax.all_to_all(padded.reshape(groups, piece_rows, -1), 'rz', 0, 0, tiled=...  10.9 us
    ppermute x4, starting transfers between devices, ring_gather(): moving = lax.ppermute(moving, 'y', right)  10.5 us
    all_to_all x1, waiting for transfers between devices, local(): lax.all_to_all(padded.reshape(groups, piece_rows, -1), 'rz', 0, 0, tiled=...  10 us
    ppermute x2, starting transfers between devices, ring_reduce(): moving = lax.ppermute(moving, 'y', left)  9.15 us
  transfers between devices with their start and end apart: 20, of which 8 were waited for; matrix products, arithmetic and copies ran while one was open for 25% of the time, Pallas kernels for 0%

profile of v4, /device:TPU:1, one launch (start us, length us, event | category | flops | bytes accessed | tf_op | source)
XLA Modules:
  0.0 186.3 jit_solution(3227241507035482498)
XLA Ops:
  1.6 3.9 %collective-permute-start = (bf16[512,128]{1,0:T(8,128)(2,1)S(1)}, bf16[512,128]{1,0:T(8,128)(2,1)S(1)}, u32[]{:S(2)}, u32[]{:S(2)}) collective-permute-start(bf16[512,128]{1,0:T(8,128)(2,1)S(1)} %constant_dynamic-slice_fusion), channel_id=1, source_target_pairs={{0,48},{48,0},{1,49},{49,1},{2,50},{50,2},{3,51},{51,3},{4,52},{52... | collective-permute-start | bytes 393224 | tf_op jit(solution)/shard_map/ppermute | solution.py:23
  15.5 2.3 %copy.78 = bf16[16,2,512,128]{3,2,0,1:T(8,128)(2,1)} copy(bf16[16,2,512,128]{3,2,1,0:T(8,128)(2,1)S(1)} %bitcast.137) | data formatting | bytes 8388608 | tf_op jit(solution)/shard_map/reshape | solution.py:116
  17.8 14.1 %all-to-all-start = ((bf16[16,2,512,128]{3,2,0,1:T(8,128)(2,1)}), bf16[16,2,512,128]{3,2,0,1:T(8,128)(2,1)}, u32[]{:S(2)}, u32[]{:S(2)}) async-start(bf16[16,2,512,128]{3,2,0,1:T(8,128)(2,1)} %copy.78), calls=%async_computation | async-start | bytes 8388608 | tf_op jit(solution)/shard_map/all_to_all | solution.py:115
  31.8 4.1 %all-to-all-done = bf16[16,2,512,128]{3,2,0,1:T(8,128)(2,1)} async-done(((bf16[16,2,512,128]{3,2,0,1:T(8,128)(2,1)}), bf16[16,2,512,128]{3,2,0,1:T(8,128)(2,1)}, u32[]{:S(2)}, u32[]{:S(2)}) %all-to-all-start) | async-done | bytes 4194336 | tf_op jit(solution)/shard_map/all_to_all | solution.py:115
  36.0 5.0 %reduce_sum.31 = bf16[16,512,128]{2,1,0:T(8,128)(2,1)} reduce(bf16[16,2,512,128]{3,2,0,1:T(8,128)(2,1)} %all-to-all-done, bf16[]{:T(256)} %constant.59.clone.1), dimensions={1}, to_apply=%region_2.3 | reduce | flops 1048576 | bytes 6291458 | tf_op jit(solution)/shard_map/reduce_sum | solution.py:118
  41.0 2.4 %fusion.1 = bf16[8,2,512,128]{3,2,1,0:T(8,128)(2,1)S(1)} fusion(s32[]{:T(128)S(6)} %select_n.55, bf16[8,2,512,128]{3,2,1,0:T(8,128)(2,1)} %bitcast.136), kind=kLoop, calls=%fused_computation.4 | loop fusion | flops 1048576 | bytes 4194308 | tf_op jit(solution)/shard_map/concatenate | solution.py:18
  45.4 4.6 %collective-permute-start.12 = (bf16[2,512,128]{2,1,0:T(8,128)(2,1)S(1)}, bf16[2,512,128]{2,1,0:T(8,128)(2,1)S(1)}, u32[]{:S(2)}, u32[]{:S(2)}) collective-permute-start(bf16[2,512,128]{2,1,0:T(8,128)(2,1)S(1)} %get-tuple-element.29), channel_id=1, source_target_pairs={{0,672},{96,0},{192,96},{288,192},{384,288},{480,384},{576,480},{6... | collective-permute-start | bytes 786440 | tf_op jit(solution)/shard_map/ppermute | solution.py:54
  50.0 4.1 %collective-permute-done.8 = bf16[2,512,128]{2,1,0:T(8,128)(2,1)S(1)} collective-permute-done((bf16[2,512,128]{2,1,0:T(8,128)(2,1)S(1)}, bf16[2,512,128]{2,1,0:T(8,128)(2,1)S(1)}, u32[]{:S(2)}, u32[]{:S(2)}) %collective-permute-start.8) | collective-permute-done | bytes 262176 | tf_op jit(solution)/shard_map/ppermute | solution.py:48
  56.1 4.6 %collective-permute-start.1 = (bf16[2,512,128]{2,1,0:T(8,128)(2,1)S(1)}, bf16[2,512,128]{2,1,0:T(8,128)(2,1)}, u32[]{:S(2)}, u32[]{:S(2)}) collective-permute-start(bf16[2,512,128]{2,1,0:T(8,128)(2,1)S(1)} %maximum_select_fusion), channel_id=1, source_target_pairs={{0,672},{96,0},{192,96},{288,192},{384,288},{480,384},{576,480},{6... | collective-permute-start | bytes 786440 | tf_op jit(solution)/shard_map/ppermute | solution.py:37
  66.7 4.6 %collective-permute-start.13 = (bf16[2,512,128]{2,1,0:T(8,128)(2,1)}, bf16[2,512,128]{2,1,0:T(8,128)(2,1)}, u32[]{:S(2)}, u32[]{:S(2)}) collective-permute-start(bf16[2,512,128]{2,1,0:T(8,128)(2,1)} %get-tuple-element.27), channel_id=1, source_target_pairs={{0,672},{96,0},{192,96},{288,192},{384,288},{480,384},{576,480},{6... | collective-permute-start | bytes 786440 | tf_op jit(solution)/shard_map/ppermute | solution.py:54
  71.3 2.3 %copy.72 = bf16[256,2048]{0,1:T(8,128)(2,1)} copy(bf16[256,2048]{1,0:T(8,128)(2,1)} %param.13) | data formatting | bytes 2097152 | tf_op args[6]
  73.6 2.3 %copy.73 = bf16[256,8,2,128]{3,0,2,1:T(8,128)(2,1)} copy(bf16[256,8,2,128]{0,3,2,1:T(8,128)(2,1)} %bitcast.138) | data formatting | bytes 2097152 | tf_op jit(solution)/shard_map/reshape | solution.py:129
  78.0 3.2 %collective-permute-start.5 = (bf16[2,512,128]{2,1,0:T(8,128)(2,1)S(1)}, bf16[2,512,128]{2,1,0:T(8,128)(2,1)S(1)}, u32[]{:S(2)}, u32[]{:S(2)}) collective-permute-start(bf16[2,512,128]{2,1,0:T(8,128)(2,1)S(1)} %collective-permute-done.4), channel_id=1, source_target_pairs={{0,96},{96,192},{192,288},{288,384},{384,480},{480,576},{576,672},... | collective-permute-start | bytes 786440 | tf_op jit(solution)/shard_map/ppermute | solution.py:33
  84.3 4.6 %collective-permute-start.14 = (bf16[2,512,128]{2,1,0:T(8,128)(2,1)S(1)}, bf16[2,512,128]{2,1,0:T(8,128)(2,1)S(1)}, u32[]{:S(2)}, u32[]{:S(2)}) collective-permute-start(bf16[2,512,128]{2,1,0:T(8,128)(2,1)S(1)} %get-tuple-element.25), channel_id=1, source_target_pairs={{0,672},{96,0},{192,96},{288,192},{384,288},{480,384},{576,480},{6... | collective-permute-start | bytes 786440 | tf_op jit(solution)/shard_map/ppermute | solution.py:56
  92.0 3.2 %collective-permute-start.6 = (bf16[2,512,128]{2,1,0:T(8,128)(2,1)S(1)}, bf16[2,512,128]{2,1,0:T(8,128)(2,1)S(1)}, u32[]{:S(2)}, u32[]{:S(2)}) collective-permute-start(bf16[2,512,128]{2,1,0:T(8,128)(2,1)S(1)} %collective-permute-done.5), channel_id=1, source_target_pairs={{0,96},{96,192},{192,288},{288,384},{384,480},{480,576},{576,672},... | collective-permute-start | bytes 786440 | tf_op jit(solution)/shard_map/ppermute | solution.py:33
  95.4 3.6 %collective-permute-start.15 = (f32[512,128]{1,0:T(8,128)S(1)}, f32[512,128]{1,0:T(8,128)S(1)}, u32[]{:S(2)}, u32[]{:S(2)}) collective-permute-start(f32[512,128]{1,0:T(8,128)S(1)} %select_bitcast_fusion), channel_id=1, source_target_pairs={{0,48},{48,0},{1,49},{49,1},{2,50},{50,2},{3,51},{51,3},{4,52},{52... | collective-permute-start | bytes 786440 | tf_op jit(solution)/shard_map/ppermute | solution.py:141
  104.7 10.9 %all-to-all-start.2 = ((f32[24,22,128]{2,1,0:T(8,128)}), f32[24,22,128]{2,1,0:T(8,128)S(1)}, u32[]{:S(2)}, u32[]{:S(2)}) async-start(f32[24,22,128]{2,1,0:T(8,128)} %reshape.331), calls=%async_computation.2 | async-start | bytes 589824 | tf_op jit(solution)/shard_map/all_to_all | solution.py:145
  118.5 10.0 %all-to-all-done.2 = f32[24,22,128]{2,1,0:T(8,128)S(1)} async-done(((f32[24,22,128]{2,1,0:T(8,128)}), f32[24,22,128]{2,1,0:T(8,128)S(1)}, u32[]{:S(2)}, u32[]{:S(2)}) %all-to-all-start.2) | async-done | bytes 270368 | tf_op jit(solution)/shard_map/all_to_all | solution.py:145
  128.6 4.8 %broadcast_in_dim.18 = bf16[2,8,2,512,128]{4,3,2,1,0:T(8,128)(2,1)} broadcast(bf16[8,2,512,128]{3,2,1,0:T(8,128)(2,1)} %bitcast_dynamic-update-slice_fusion), dimensions={1,2,3,4} | broadcast | bytes 6291456 | tf_op jit(solution)/shard_map/broadcast_in_dim | solution.py:123
  133.4 12.0 %all-to-all-start.1 = ((bf16[2,8,2,512,128]{4,3,2,1,0:T(8,128)(2,1)}), bf16[2,8,2,512,128]{4,3,2,1,0:T(8,128)(2,1)}, u32[]{:S(2)}, u32[]{:S(2)}) async-start(bf16[2,8,2,512,128]{4,3,2,1,0:T(8,128)(2,1)} %broadcast_in_dim.18), calls=%async_computation.1 | async-start | bytes 8388608 | tf_op jit(solution)/shard_map/all_to_all | solution.py:122
  145.5 4.1 %all-to-all-done.1 = bf16[2,8,2,512,128]{4,3,2,1,0:T(8,128)(2,1)} async-done(((bf16[2,8,2,512,128]{4,3,2,1,0:T(8,128)(2,1)}), bf16[2,8,2,512,128]{4,3,2,1,0:T(8,128)(2,1)}, u32[]{:S(2)}, u32[]{:S(2)}) %all-to-all-start.1) | async-done | bytes 4194336 | tf_op jit(solution)/shard_map/all_to_all | solution.py:122
  150.4 6.0 %all-to-all-start.3 = ((f32[48,22,128]{2,1,0:T(8,128)}), f32[48,22,128]{2,1,0:T(8,128)S(1)}, u32[]{:S(2)}, u32[]{:S(2)}) async-start(f32[48,22,128]{2,1,0:T(8,128)} %broadcast_in_dim.19), calls=%async_computation.3 | async-start | bytes 1179648 | tf_op jit(solution)/shard_map/all_to_all | solution.py:149
  156.4 3.8 %fusion.3 = bf16[256,2,512]{2,0,1:T(8,128)(2,1)S(1)} fusion(bf16[2,8,2,512,128]{4,3,2,1,0:T(8,128)(2,1)} %all-to-all-done.1, s32[]{:T(128)S(6)} %select_n.55, bf16[256,8,2,128]{3,0,2,1:T(8,128)(2,1)} %copy.73), kind=kOutput, calls=%fused_computation.16 | convolution fusion | flops 1076101120 | bytes 5767172 | tf_op jit(solution)/shard_map/toxc,poxrc->tpr/dot_general | solution.py:130
  172.4 12.7 %all-to-all-done.3 = f32[48,22,128]{2,1,0:T(8,128)S(1)} async-done(((f32[48,22,128]{2,1,0:T(8,128)}), f32[48,22,128]{2,1,0:T(8,128)S(1)}, u32[]{:S(2)}, u32[]{:S(2)}) %all-to-all-start.3) | async-done | bytes 540704 | tf_op jit(solution)/shard_map/all_to_all | solution.py:149
  (86 shorter events, 52.0 us)
Async XLA Ops:
  0.6 11.5 %copy-start = (bf16[256,1024]{1,0:T(8,128)(2,1)S(1)}, bf16[256,1024]{1,0:T(8,128)(2,1)}, u32[]{:S(2)}) copy-start(bf16[256,1024]{1,0:T(8,128)(2,1)} %param.9) | copy-start | bytes 1572868
  1.6 41.8 %collective-permute-start = (bf16[512,128]{1,0:T(8,128)(2,1)S(1)}, bf16[512,128]{1,0:T(8,128)(2,1)S(1)}, u32[]{:S(2)}, u32[]{:S(2)}) collective-permute-start(bf16[512,128]{1,0:T(8,128)(2,1)S(1)} %constant_dynamic-slice_fusion), channel_id=1, source_target_pairs={{0,48},{48,0},{1,49},{49,1},{2,50},{50,2},{3,51},{51,3},{4,52},{52... | collective-permute-start | bytes 393224 | tf_op jit(solution)/shard_map/ppermute | solution.py:23
  8.2 3.9 %copy-start.2 = (bf16[256,1024]{0,1:T(8,128)(2,1)}, bf16[256,1024]{0,1:T(8,128)(2,1)S(1)}, u32[]{:S(2)}) copy-start(bf16[256,1024]{0,1:T(8,128)(2,1)S(1)} %copy.110) | copy-start | bytes 1572868
  17.8 18.2 %all-to-all-start = ((bf16[16,2,512,128]{3,2,0,1:T(8,128)(2,1)}), bf16[16,2,512,128]{3,2,0,1:T(8,128)(2,1)}, u32[]{:S(2)}, u32[]{:S(2)}) async-start(bf16[16,2,512,128]{3,2,0,1:T(8,128)(2,1)} %copy.78), calls=%async_computation | async-start | bytes 8388608 | tf_op jit(solution)/shard_map/all_to_all | solution.py:115
  43.5 10.6 %collective-permute-start.8 = (bf16[2,512,128]{2,1,0:T(8,128)(2,1)S(1)}, bf16[2,512,128]{2,1,0:T(8,128)(2,1)S(1)}, u32[]{:S(2)}, u32[]{:S(2)}) collective-permute-start(bf16[2,512,128]{2,1,0:T(8,128)(2,1)S(1)} %get-tuple-element.28), channel_id=1, source_target_pairs={{0,96},{96,192},{192,288},{288,384},{384,480},{480,576},{576,672},... | collective-permute-start | bytes 786440 | tf_op jit(solution)/shard_map/ppermute | solution.py:48
  45.4 17.2 %collective-permute-start.12 = (bf16[2,512,128]{2,1,0:T(8,128)(2,1)S(1)}, bf16[2,512,128]{2,1,0:T(8,128)(2,1)S(1)}, u32[]{:S(2)}, u32[]{:S(2)}) collective-permute-start(bf16[2,512,128]{2,1,0:T(8,128)(2,1)S(1)} %get-tuple-element.29), channel_id=1, source_target_pairs={{0,672},{96,0},{192,96},{288,192},{384,288},{480,384},{576,480},{6... | collective-permute-start | bytes 786440 | tf_op jit(solution)/shard_map/ppermute | solution.py:54
  54.2 9.7 %collective-permute-start.9 = (bf16[2,512,128]{2,1,0:T(8,128)(2,1)S(1)}, bf16[2,512,128]{2,1,0:T(8,128)(2,1)S(1)}, u32[]{:S(2)}, u32[]{:S(2)}) collective-permute-start(bf16[2,512,128]{2,1,0:T(8,128)(2,1)S(1)} %fusion.20), channel_id=1, source_target_pairs={{0,96},{96,192},{192,288},{288,384},{384,480},{480,576},{576,672},... | collective-permute-start | bytes 786440 | tf_op jit(solution)/shard_map/ppermute | solution.py:48
  56.1 19.7 %collective-permute-start.1 = (bf16[2,512,128]{2,1,0:T(8,128)(2,1)S(1)}, bf16[2,512,128]{2,1,0:T(8,128)(2,1)}, u32[]{:S(2)}, u32[]{:S(2)}) collective-permute-start(bf16[2,512,128]{2,1,0:T(8,128)(2,1)S(1)} %maximum_select_fusion), channel_id=1, source_target_pairs={{0,672},{96,0},{192,96},{288,192},{384,288},{480,384},{576,480},{6... | collective-permute-start | bytes 786440 | tf_op jit(solution)/shard_map/ppermute | solution.py:37
  60.7 17.3 %collective-permute-start.4 = (bf16[2,512,128]{2,1,0:T(8,128)(2,1)S(1)}, bf16[2,512,128]{2,1,0:T(8,128)(2,1)S(1)}, u32[]{:S(2)}, u32[]{:S(2)}) collective-permute-start(bf16[2,512,128]{2,1,0:T(8,128)(2,1)S(1)} %maximum_select_fusion), channel_id=1, source_target_pairs={{0,96},{96,192},{192,288},{288,384},{384,480},{480,576},{576,672},... | collective-permute-start | bytes 786440 | tf_op jit(solution)/shard_map/ppermute | solution.py:33
  64.8 16.3 %collective-permute-start.10 = (bf16[2,512,128]{2,1,0:T(8,128)(2,1)}, bf16[2,512,128]{2,1,0:T(8,128)(2,1)}, u32[]{:S(2)}, u32[]{:S(2)}) collective-permute-start(bf16[2,512,128]{2,1,0:T(8,128)(2,1)} %get-tuple-element.26), channel_id=1, source_target_pairs={{0,96},{96,192},{192,288},{288,384},{384,480},{480,576},{576,672},... | collective-permute-start | bytes 786440 | tf_op jit(solution)/shard_map/ppermute | solution.py:48
  66.7 14.4 %collective-permute-start.13 = (bf16[2,512,128]{2,1,0:T(8,128)(2,1)}, bf16[2,512,128]{2,1,0:T(8,128)(2,1)}, u32[]{:S(2)}, u32[]{:S(2)}) collective-permute-start(bf16[2,512,128]{2,1,0:T(8,128)(2,1)} %get-tuple-element.27), channel_id=1, source_target_pairs={{0,672},{96,0},{192,96},{288,192},{384,288},{480,384},{576,480},{6... | collective-permute-start | bytes 786440 | tf_op jit(solution)/shard_map/ppermute | solution.py:54
  75.9 14.0 %collective-permute-start.2 = (bf16[2,512,128]{2,1,0:T(8,128)(2,1)}, bf16[2,512,128]{2,1,0:T(8,128)(2,1)S(1)}, u32[]{:S(2)}, u32[]{:S(2)}) collective-permute-start(bf16[2,512,128]{2,1,0:T(8,128)(2,1)} %collective-permute-done.1), channel_id=1, source_target_pairs={{0,672},{96,0},{192,96},{288,192},{384,288},{480,384},{576,480},{6... | collective-permute-start | bytes 786440 | tf_op jit(solution)/shard_map/ppermute | solution.py:37
  78.0 14.0 %collective-permute-start.5 = (bf16[2,512,128]{2,1,0:T(8,128)(2,1)S(1)}, bf16[2,512,128]{2,1,0:T(8,128)(2,1)S(1)}, u32[]{:S(2)}, u32[]{:S(2)}) collective-permute-start(bf16[2,512,128]{2,1,0:T(8,128)(2,1)S(1)} %collective-permute-done.4), channel_id=1, source_target_pairs={{0,96},{96,192},{192,288},{288,384},{384,480},{480,576},{576,672},... | collective-permute-start | bytes 786440 | tf_op jit(solution)/shard_map/ppermute | solution.py:33
  82.3 12.8 %collective-permute-start.11 = (bf16[2,512,128]{2,1,0:T(8,128)(2,1)S(1)}, bf16[2,512,128]{2,1,0:T(8,128)(2,1)S(1)}, u32[]{:S(2)}, u32[]{:S(2)}) collective-permute-start(bf16[2,512,128]{2,1,0:T(8,128)(2,1)S(1)} %get-tuple-element.24), channel_id=1, source_target_pairs={{0,96},{96,192},{192,288},{288,384},{384,480},{480,576},{576,672},... | collective-permute-start | bytes 786440 | tf_op jit(solution)/shard_map/ppermute | solution.py:50
  84.3 10.9 %collective-permute-start.14 = (bf16[2,512,128]{2,1,0:T(8,128)(2,1)S(1)}, bf16[2,512,128]{2,1,0:T(8,128)(2,1)S(1)}, u32[]{:S(2)}, u32[]{:S(2)}) collective-permute-start(bf16[2,512,128]{2,1,0:T(8,128)(2,1)S(1)} %get-tuple-element.25), channel_id=1, source_target_pairs={{0,672},{96,0},{192,96},{288,192},{384,288},{480,384},{576,480},{6... | collective-permute-start | bytes 786440 | tf_op jit(solution)/shard_map/ppermute | solution.py:56
  89.9 12.7 %collective-permute-start.3 = (bf16[2,512,128]{2,1,0:T(8,128)(2,1)S(1)}, bf16[2,512,128]{2,1,0:T(8,128)(2,1)S(1)}, u32[]{:S(2)}, u32[]{:S(2)}) collective-permute-start(bf16[2,512,128]{2,1,0:T(8,128)(2,1)S(1)} %collective-permute-done.2), channel_id=1, source_target_pairs={{0,672},{96,0},{192,96},{288,192},{384,288},{480,384},{576,480},{6... | collective-permute-start | bytes 786440 | tf_op jit(solution)/shard_map/ppermute | solution.py:37
  92.0 8.3 %collective-permute-start.6 = (bf16[2,512,128]{2,1,0:T(8,128)(2,1)S(1)}, bf16[2,512,128]{2,1,0:T(8,128)(2,1)S(1)}, u32[]{:S(2)}, u32[]{:S(2)}) collective-permute-start(bf16[2,512,128]{2,1,0:T(8,128)(2,1)S(1)} %collective-permute-done.5), channel_id=1, source_target_pairs={{0,96},{96,192},{192,288},{288,384},{384,480},{480,576},{576,672},... | collective-permute-start | bytes 786440 | tf_op jit(solution)/shard_map/ppermute | solution.py:33
  95.4 7.7 %collective-permute-start.15 = (f32[512,128]{1,0:T(8,128)S(1)}, f32[512,128]{1,0:T(8,128)S(1)}, u32[]{:S(2)}, u32[]{:S(2)}) collective-permute-start(f32[512,128]{1,0:T(8,128)S(1)} %select_bitcast_fusion), channel_id=1, source_target_pairs={{0,48},{48,0},{1,49},{49,1},{2,50},{50,2},{3,51},{51,3},{4,52},{52... | collective-permute-start | bytes 786440 | tf_op jit(solution)/shard_map/ppermute | solution.py:141
  100.3 15.3 %collective-permute-start.7 = (bf16[2,512,128]{2,1,0:T(8,128)(2,1)S(1)}, bf16[2,512,128]{2,1,0:T(8,128)(2,1)S(1)}, u32[]{:S(2)}, u32[]{:S(2)}) collective-permute-start(bf16[2,512,128]{2,1,0:T(8,128)(2,1)S(1)} %collective-permute-done.6), channel_id=1, source_target_pairs={{0,96},{96,192},{192,288},{288,384},{384,480},{480,576},{576,672},... | collective-permute-start | bytes 786440 | tf_op jit(solution)/shard_map/ppermute | solution.py:33
  104.7 23.8 %all-to-all-start.2 = ((f32[24,22,128]{2,1,0:T(8,128)}), f32[24,22,128]{2,1,0:T(8,128)S(1)}, u32[]{:S(2)}, u32[]{:S(2)}) async-start(f32[24,22,128]{2,1,0:T(8,128)} %reshape.331), calls=%async_computation.2 | async-start | bytes 589824 | tf_op jit(solution)/shard_map/all_to_all | solution.py:145
  133.4 16.1 %all-to-all-start.1 = ((bf16[2,8,2,512,128]{4,3,2,1,0:T(8,128)(2,1)}), bf16[2,8,2,512,128]{4,3,2,1,0:T(8,128)(2,1)}, u32[]{:S(2)}, u32[]{:S(2)}) async-start(bf16[2,8,2,512,128]{4,3,2,1,0:T(8,128)(2,1)} %broadcast_in_dim.18), calls=%async_computation.1 | async-start | bytes 8388608 | tf_op jit(solution)/shard_map/all_to_all | solution.py:122
  150.4 34.7 %all-to-all-start.3 = ((f32[48,22,128]{2,1,0:T(8,128)}), f32[48,22,128]{2,1,0:T(8,128)S(1)}, u32[]{:S(2)}, u32[]{:S(2)}) async-start(f32[48,22,128]{2,1,0:T(8,128)} %broadcast_in_dim.19), calls=%async_computation.3 | async-start | bytes 1179648 | tf_op jit(solution)/shard_map/all_to_all | solution.py:149
  160.5 3.2 %copy-start.8 = (bf16[8,256,128]{1,2,0:T(8,128)(2,1)S(1)}, bf16[8,256,128]{1,2,0:T(8,128)(2,1)}, u32[]{:S(2)}) copy-start(bf16[8,256,128]{1,2,0:T(8,128)(2,1)} %copy-done.7) | copy-start | bytes 1572868
  165.9 3.3 %copy-start.3 = (bf16[256,1024]{0,1:T(8,128)(2,1)S(1)}, bf16[256,1024]{0,1:T(8,128)(2,1)}, u32[]{:S(2)}) copy-start(bf16[256,1024]{0,1:T(8,128)(2,1)} %copy-done.2) | copy-start | bytes 1572868
  (6 other events, 11.7 us)

commit v5 on v4

--- a/solution.py
+++ b/solution.py
@@ -112,27 +112,27 @@
         )
         / math.sqrt(total_tokens)
     ).astype(jnp.bfloat16)
-    pair = lax.all_to_all(
-        term.reshape(shard_count, cores, part_rows, -1), "core", 1, 1, tiled=True
-    )
-    pair_sum = jnp.sum(pair.astype(jnp.float32), axis=1).astype(jnp.bfloat16)
+    halves = term.reshape(shard_count, cores, part_rows, -1)
+    own_half = jnp.where(core == 0, halves[:, 0], halves[:, 1])
+    sent_half = jnp.where(core == 0, halves[:, 1], halves[:, 0])
+    got_half = lax.ppermute(sent_half, "core", [(0, 1), (1, 0)])
+    pair_sum = (own_half.astype(jnp.float32) + got_half.astype(jnp.float32)).astype(jnp.bfloat16)
     pair_rot = rotate(pair_sum.reshape(ys, xls, part_rows, -1), y_at, 0)
     weight_pair, pair_rot = lax.optimization_barrier((weight_pair, pair_rot))
     weight_ring = ring_gather(weight_pair, ys)
-    weight_all = lax.all_to_all(
-        jnp.broadcast_to(weight_ring[None], (cores,) + weight_ring.shape),
-        "core",
-        0,
-        0,
-        tiled=True,
+    weight_other = lax.ppermute(weight_ring, "core", [(0, 1), (1, 0)])
+    grad_rot = rotate(grad_out.reshape(tok_rows, ys, xls, -1), y_at, 1)
+    own_cols = jnp.einsum(
+        "toxc,oxrc->tr", grad_rot, weight_ring, preferred_element_type=jnp.float32
     )
-    grad_rot = rotate(grad_out.reshape(tok_rows, ys, xls, -1), y_at, 1)
-    grad_att32 = jnp.einsum(
-        "toxc,poxrc->tpr",
-        grad_rot,
-        weight_all,
-        preferred_element_type=jnp.float32,
-    ).reshape(tok_rows, q_width)
+    other_cols = jnp.einsum(
+        "toxc,oxrc->tr", grad_rot, weight_other, preferred_element_type=jnp.float32
+    )
+    grad_att32 = jnp.where(
+        core == 0,
+        jnp.concatenate([own_cols, other_cols], axis=1),
+        jnp.concatenate([other_cols, own_cols], axis=1),
+    )
     grad_att = grad_att32.astype(jnp.bfloat16)
     grad_h = grad_att.reshape(seq_count, SEQ, HEADS, HEAD_DIM)
     y_sum = ring_reduce(pair_rot, ys)

time: 188 us -> 184 us (0.979)
  local copies, waits for them, and re-layouts: 28.4 us -> 17.1 us
  waiting for transfers between devices: 38.1 us -> 48.9 us
  starting transfers between devices: 91.3 us -> 86.4 us
    all_to_all x2 -> x0, starting transfers between devices: 26.1 us -> none  [the longest x1 14.1 us: local(): lax.all_to_all(term.reshape(shard_count, cores, part_rows, -1), 'core', 1...]
    ppermute x0 -> x2, starting transfers between devices: none -> 19.2 us  [the longest x1 12.4 us: local(): got_half = lax.ppermute(sent_half, 'core', [(0, 1), (1, 0)])]
    all_to_all x2 -> x0, waiting for transfers between devices: 8.22 us -> none  [the longest x1 4.13 us: local(): lax.all_to_all(term.reshape(shard_count, cores, part_rows, -1), 'core', 1...]
    ppermute x1, waiting for transfers between devices: 0.39 us -> 6.22 us  [local(): shard_sum = keep + lax.ppermute(send, 'xl', [(0, 1), (1, 0)])]
    ppermute x3, starting transfers between devices: 8.8 us -> 14.5 us  [ring_gather(): moving = lax.ppermute(moving, 'y', left)]
    all_to_all x1, starting transfers between devices: 6 us -> 11.1 us  [local(): lax.all_to_all(jnp.broadcast_to(piece_sum[None], (groups * cores,) + piec...]
    ppermute x1, waiting for transfers between devices: 0.01 us -> 5.05 us  [swap_in(): other = lax.ppermute(block, 'xl', [(0, 1), (1, 0)])]
    reduce_sum x1 -> x0, other arithmetic: 4.99 us -> none  [local(): pair_sum = jnp.sum(pair.astype(jnp.float32), axis=1).astype(jnp.bfloat16)]
  transfers between devices with their start and end apart: 20 -> 20, of which waited for: 8 -> 9; matrix products, arithmetic and copies ran while one was open for 25% -> 13% of each run, Pallas kernels for 0% -> 0%
where the time goes in v5:
time: 184 us; the launch traced here: 182 us
  starting transfers between devices  86.4 us (47%)
  waiting for transfers between devices  48.9 us (27%)
  matrix products  17.5 us (10%)
  local copies, waits for them, and re-layouts  17.1 us (9%)
  other arithmetic  10.6 us (6%)
    all_to_all x1, waiting for transfers between devices, local(): lax.all_to_all(jnp.broadcast_to(piece_sum[None], (groups * cores,) + piec...  15.6 us
    ppermute x3, starting transfers between devices, ring_gather(): moving = lax.ppermute(moving, 'y', left)  14.5 us
    ppermute x1, starting transfers between devices, local(): got_half = lax.ppermute(sent_half, 'core', [(0, 1), (1, 0)])  12.4 us
    all_to_all x1, starting transfers between devices, local(): lax.all_to_all(jnp.broadcast_to(piece_sum[None], (groups * cores,) + piec...  11.1 us
    unnamed x33, local copies, waits for them, and re-layouts  9.88 us
    all_to_all x1, waiting for transfers between devices, local(): lax.all_to_all(padded.reshape(groups, piece_rows, -1), 'rz', 0, 0, tiled=...  9.44 us
    all_to_all x1, starting transfers between devices, local(): lax.all_to_all(padded.reshape(groups, piece_rows, -1), 'rz', 0, 0, tiled=...  9.38 us
    ppermute x2, starting transfers between devices, ring_reduce(): moving = lax.ppermute(moving, 'y', left)  7.93 us
  transfers between devices with their start and end apart: 20, of which 9 were waited for; matrix products, arithmetic and copies ran while one was open for 13% of the time, Pallas kernels for 0%

profile of v5, /device:TPU:1, one launch (start us, length us, event | category | flops | bytes accessed | tf_op | source)
XLA Modules:
  0.0 181.7 jit_solution(13258241033588336612)
XLA Ops:
  10.0 3.2 %multiply_convert_fusion = bf16[1024,16,128]{2,0,1:T(8,128)(2,1)} fusion(bf16[256,1024,1]{0,1,2:T(8,128)(2,1)S(1)} %bitcast.167, bf16[256,2048]{1,0:T(8,128)(2,1)S(1)} %copy-done.5), kind=kOutput, calls=%fused_computation.1 | convolution fusion | flops 1077936128 | bytes 5767168 | tf_op jit(solution)/shard_map/tr,tjc->jrc/dot_general | solution.py:107
  13.3 2.5 %fusion.2 = bf16[16,512,128]{2,1,0:T(8,128)(2,1)S(1)} fusion(pred[]{:T(512)S(6)} %eq.86, bf16[16,2,512,128]{3,2,1,0:T(8,128)(2,1)} %bitcast.154), kind=kLoop, calls=%fused_computation.7 | loop fusion | flops 1048576 | bytes 6291457 | tf_op jit(solution)/shard_map/jit(_where)/select_n | solution.py:117
  15.8 12.4 %collective-permute-start.1 = (bf16[16,512,128]{2,1,0:T(8,128)(2,1)S(1)}, bf16[16,512,128]{2,1,0:T(8,128)(2,1)}, u32[]{:S(2)}, u32[]{:S(2)}) collective-permute-start(bf16[16,512,128]{2,1,0:T(8,128)(2,1)S(1)} %fusion.2), channel_id=1, source_target_pairs={{0,1},{1,0},{2,3},{3,2},{4,5},{5,4},{6,7},{7,6},{8,9},{9,8},{10,11... | collective-permute-start | bytes 6291464 | tf_op jit(solution)/shard_map/ppermute | solution.py:118
  30.2 5.0 %collective-permute-done = bf16[512,128]{1,0:T(8,128)(2,1)S(1)} collective-permute-done((bf16[512,128]{1,0:T(8,128)(2,1)S(1)}, bf16[512,128]{1,0:T(8,128)(2,1)S(1)}, u32[]{:S(2)}, u32[]{:S(2)}) %collective-permute-start) | collective-permute-done | bytes 131104 | tf_op jit(solution)/shard_map/ppermute | solution.py:23
  35.3 3.7 %fusion.1 = bf16[16,512,128]{2,1,0:T(8,128)(2,1)S(1)} fusion(bf16[16,512,128]{2,1,0:T(8,128)(2,1)} %collective-permute-done.1, pred[]{:T(512)S(6)} %eq.86, bf16[16,2,512,128]{3,2,1,0:T(8,128)(2,1)} %bitcast.155), kind=kLoop, calls=%fused_computation.5 | loop fusion | flops 5242880 | bytes 8388609 | tf_op jit(solution)/shard_map/convert_element_type | solution.py:119
  43.6 4.6 %collective-permute-start.2 = (bf16[2,512,128]{2,1,0:T(8,128)(2,1)S(1)}, bf16[2,512,128]{2,1,0:T(8,128)(2,1)S(1)}, u32[]{:S(2)}, u32[]{:S(2)}) collective-permute-start(bf16[2,512,128]{2,1,0:T(8,128)(2,1)S(1)} %maximum_select_fusion.1), channel_id=1, source_target_pairs={{0,672},{96,0},{192,96},{288,192},{384,288},{480,384},{576,480},{6... | collective-permute-start | bytes 786440 | tf_op jit(solution)/shard_map/ppermute | solution.py:37
  48.2 3.4 %collective-permute-start.14 = (bf16[2,512,128]{2,1,0:T(8,128)(2,1)S(1)}, bf16[2,512,128]{2,1,0:T(8,128)(2,1)S(1)}, u32[]{:S(2)}, u32[]{:S(2)}) collective-permute-start(bf16[2,512,128]{2,1,0:T(8,128)(2,1)S(1)} %get-tuple-element.29), channel_id=1, source_target_pairs={{0,672},{96,0},{192,96},{288,192},{384,288},{480,384},{576,480},{6... | collective-permute-start | bytes 786440 | tf_op jit(solution)/shard_map/ppermute | solution.py:54
  57.5 4.6 %collective-permute-start.3 = (bf16[2,512,128]{2,1,0:T(8,128)(2,1)S(1)}, bf16[2,512,128]{2,1,0:T(8,128)(2,1)S(1)}, u32[]{:S(2)}, u32[]{:S(2)}) collective-permute-start(bf16[2,512,128]{2,1,0:T(8,128)(2,1)S(1)} %collective-permute-done.2), channel_id=1, source_target_pairs={{0,672},{96,0},{192,96},{288,192},{384,288},{480,384},{576,480},{6... | collective-permute-start | bytes 786440 | tf_op jit(solution)/shard_map/ppermute | solution.py:37
  65.7 5.3 %collective-permute-start.4 = (bf16[2,512,128]{2,1,0:T(8,128)(2,1)S(1)}, bf16[2,512,128]{2,1,0:T(8,128)(2,1)S(1)}, u32[]{:S(2)}, u32[]{:S(2)}) collective-permute-start(bf16[2,512,128]{2,1,0:T(8,128)(2,1)S(1)} %collective-permute-done.3), channel_id=1, source_target_pairs={{0,672},{96,0},{192,96},{288,192},{384,288},{480,384},{576,480},{6... | collective-permute-start | bytes 786440 | tf_op jit(solution)/shard_map/ppermute | solution.py:37
  73.2 4.6 %collective-permute-start.15 = (bf16[2,512,128]{2,1,0:T(8,128)(2,1)S(1)}, bf16[2,512,128]{2,1,0:T(8,128)(2,1)S(1)}, u32[]{:S(2)}, u32[]{:S(2)}) collective-permute-start(bf16[2,512,128]{2,1,0:T(8,128)(2,1)S(1)} %get-tuple-element.27), channel_id=1, source_target_pairs={{0,672},{96,0},{192,96},{288,192},{384,288},{480,384},{576,480},{6... | collective-permute-start | bytes 786440 | tf_op jit(solution)/shard_map/ppermute | solution.py:54
  81.1 4.9 %collective-permute-done.8 = bf16[2,512,128]{2,1,0:T(8,128)(2,1)S(1)} collective-permute-done((bf16[2,512,128]{2,1,0:T(8,128)(2,1)S(1)}, bf16[2,512,128]{2,1,0:T(8,128)(2,1)S(1)}, u32[]{:S(2)}, u32[]{:S(2)}) %collective-permute-start.8) | collective-permute-done | bytes 262176 | tf_op jit(solution)/shard_map/ppermute | solution.py:33
  88.9 6.8 %collective-permute-start.9 = (bf16[8,2,512,128]{3,2,1,0:T(8,128)(2,1)}, bf16[8,2,512,128]{3,2,1,0:T(8,128)(2,1)}, u32[]{:S(2)}, u32[]{:S(2)}) collective-permute-start(bf16[8,2,512,128]{3,2,1,0:T(8,128)(2,1)} %bitcast_dynamic-update-slice_fusion), channel_id=1, source_target_pairs={{0,1},{1,0},{2,3},{3,2},{4,5},{5,4},{6,7},{7,6},{8,9},{9,8},{10,11... | collective-permute-start | bytes 6291464 | tf_op jit(solution)/shard_map/ppermute | solution.py:123
  97.8 4.7 %collective-permute-start.16 = (bf16[2,512,128]{2,1,0:T(8,128)(2,1)S(1)}, bf16[2,512,128]{2,1,0:T(8,128)(2,1)S(1)}, u32[]{:S(2)}, u32[]{:S(2)}) collective-permute-start(bf16[2,512,128]{2,1,0:T(8,128)(2,1)S(1)} %get-tuple-element.25), channel_id=1, source_target_pairs={{0,672},{96,0},{192,96},{288,192},{384,288},{480,384},{576,480},{6... | collective-permute-start | bytes 786440 | tf_op jit(solution)/shard_map/ppermute | solution.py:56
  102.5 4.4 %collective-permute-done.13 = bf16[2,512,128]{2,1,0:T(8,128)(2,1)S(1)} collective-permute-done((bf16[2,512,128]{2,1,0:T(8,128)(2,1)S(1)}, bf16[2,512,128]{2,1,0:T(8,128)(2,1)S(1)}, u32[]{:S(2)}, u32[]{:S(2)}) %collective-permute-start.13) | collective-permute-done | bytes 262176 | tf_op jit(solution)/shard_map/ppermute | solution.py:50
  108.1 2.4 %collective-permute-start.17 = (f32[512,128]{1,0:T(8,128)S(1)}, f32[512,128]{1,0:T(8,128)S(1)}, u32[]{:S(2)}, u32[]{:S(2)}) collective-permute-start(f32[512,128]{1,0:T(8,128)S(1)} %select_bitcast_fusion), channel_id=1, source_target_pairs={{0,48},{48,0},{1,49},{49,1},{2,50},{50,2},{3,51},{51,3},{4,52},{52... | collective-permute-start | bytes 786440 | tf_op jit(solution)/shard_map/ppermute | solution.py:141
  110.4 6.2 %collective-permute-done.17 = f32[512,128]{1,0:T(8,128)S(1)} collective-permute-done((f32[512,128]{1,0:T(8,128)S(1)}, f32[512,128]{1,0:T(8,128)S(1)}, u32[]{:S(2)}, u32[]{:S(2)}) %collective-permute-start.17) | collective-permute-done | bytes 262176 | tf_op jit(solution)/shard_map/ppermute | solution.py:141
  117.4 9.4 %all-to-all-start = ((f32[24,22,128]{2,1,0:T(8,128)}), f32[24,22,128]{2,1,0:T(8,128)S(1)}, u32[]{:S(2)}, u32[]{:S(2)}) async-start(f32[24,22,128]{2,1,0:T(8,128)} %reshape.341), calls=%async_computation | async-start | bytes 589824 | tf_op jit(solution)/shard_map/all_to_all | solution.py:145
  128.0 2.3 %convolution_bitcast_fusion.1 = bf16[256,512]{1,0:T(8,128)(2,1)S(1)} fusion(bf16[8,2,512,128]{3,2,1,0:T(8,128)(2,1)} %bitcast_dynamic-update-slice_fusion, s32[]{:T(128)S(6)} %select_n.85, bf16[256,8,2,128]{3,0,2,1:T(8,128)(2,1)S(1)} %copy.86), kind=kOutput, calls=%fused_computation.22 | convolution fusion | flops 537395200 | bytes 3407876 | tf_op jit(solution)/shard_map/toxc,oxrc->tr/dot_general | solution.py:125
  130.4 9.4 %all-to-all-done = f32[24,22,128]{2,1,0:T(8,128)S(1)} async-done(((f32[24,22,128]{2,1,0:T(8,128)}), f32[24,22,128]{2,1,0:T(8,128)S(1)}, u32[]{:S(2)}, u32[]{:S(2)}) %all-to-all-start) | async-done | bytes 270368 | tf_op jit(solution)/shard_map/all_to_all | solution.py:145
  140.7 11.1 %all-to-all-start.1 = ((f32[48,22,128]{2,1,0:T(8,128)}), f32[48,22,128]{2,1,0:T(8,128)S(1)}, u32[]{:S(2)}, u32[]{:S(2)}) async-start(f32[48,22,128]{2,1,0:T(8,128)} %broadcast_in_dim.12), calls=%async_computation.1 | async-start | bytes 1179648 | tf_op jit(solution)/shard_map/all_to_all | solution.py:149
  151.9 2.3 %convolution_bitcast_fusion = bf16[256,512]{1,0:T(8,128)(2,1)S(1)} fusion(bf16[8,2,512,128]{3,2,1,0:T(8,128)(2,1)} %collective-permute-done.9, s32[]{:T(128)S(6)} %select_n.85, bf16[256,8,2,128]{3,0,2,1:T(8,128)(2,1)S(1)} %copy.86), kind=kOutput, calls=%fused_computation.21 | convolution fusion | flops 537395200 | bytes 3407876 | tf_op jit(solution)/shard_map/toxc,oxrc->tr/dot_general | solution.py:128
  154.8 2.3 %convolution_convert_fusion.2 = bf16[8,128,256]{2,1,0:T(8,128)(2,1)S(1)} fusion(bf16[256,8,128]{0,2,1:T(8,128)(2,1)S(1)} %copy.102, f32[8,256,256]{1,2,0:T(8,128)} %get-tuple-element.33, f32[8,256]{1,0:T(8,128)S(1)} %get-tuple-element.32), kind=kOutput, calls=%fused_computation.19 | convolution fusion | flops 135528448 | bytes 3153920 | tf_op jit(solution)/shard_map/bhqk,bqhd->bkhd/dot_general | solution.py:169
  159.8 2.3 %multiply_convert_fusion.1 = bf16[8,256,256]{1,2,0:T(8,128)(2,1)S(1)} fusion(bf16[256,8,128]{0,2,1:T(8,128)(2,1)} %copy-done.8, f32[8,256]{1,0:T(8,128)S(1)} %multiply_reduce_fusion, f32[8,256,256]{1,2,0:T(8,128)} %get-tuple-element.33, f32[8,256]{1,0:T(8,128)S(1)} %get-tuple-element.32, bf16[256,1024]{1,0:T(8,128)(2,1)S(1)} %copy-done), kind=kOutput, calls=%fused_computation.13 | convolution fusion | flops 136839168 | bytes 4210688 | tf_op jit(solution)/shard_map/bqhd,bkhd->bhqk/dot_general | solution.py:162
  164.9 15.6 %all-to-all-done.1 = f32[48,22,128]{2,1,0:T(8,128)S(1)} async-done(((f32[48,22,128]{2,1,0:T(8,128)}), f32[48,22,128]{2,1,0:T(8,128)S(1)}, u32[]{:S(2)}, u32[]{:S(2)}) %all-to-all-start.1) | async-done | bytes 540704 | tf_op jit(solution)/shard_map/all_to_all | solution.py:149
  (90 shorter events, 47.1 us)
Async XLA Ops:
  0.6 6.5 %copy-start = (bf16[256,1024]{1,0:T(8,128)(2,1)S(1)}, bf16[256,1024]{1,0:T(8,128)(2,1)}, u32[]{:S(2)}) copy-start(bf16[256,1024]{1,0:T(8,128)(2,1)} %param.9) | copy-start | bytes 1572868
  3.3 3.8 %copy-start.1 = (bf16[256,1024]{0,1:T(8,128)(2,1)}, bf16[256,1024]{0,1:T(8,128)(2,1)S(1)}, u32[]{:S(2)}) copy-start(bf16[256,1024]{0,1:T(8,128)(2,1)S(1)} %copy.124) | copy-start | bytes 1572868
  13.3 14.9 %copy-start.9 = (bf16[1024,128]{1,0:T(8,128)(2,1)S(1)}, bf16[1024,128]{1,0:T(8,128)(2,1)}, u32[]{:S(2)}) copy-start(bf16[1024,128]{1,0:T(8,128)(2,1)} %param.12) | copy-start | bytes 786436
  15.8 19.5 %collective-permute-start.1 = (bf16[16,512,128]{2,1,0:T(8,128)(2,1)S(1)}, bf16[16,512,128]{2,1,0:T(8,128)(2,1)}, u32[]{:S(2)}, u32[]{:S(2)}) collective-permute-start(bf16[16,512,128]{2,1,0:T(8,128)(2,1)S(1)} %fusion.2), channel_id=1, source_target_pairs={{0,1},{1,0},{2,3},{3,2},{4,5},{5,4},{6,7},{7,6},{8,9},{9,8},{10,11... | collective-permute-start | bytes 6291464 | tf_op jit(solution)/shard_map/ppermute | solution.py:118
  28.2 7.0 %collective-permute-start = (bf16[512,128]{1,0:T(8,128)(2,1)S(1)}, bf16[512,128]{1,0:T(8,128)(2,1)S(1)}, u32[]{:S(2)}, u32[]{:S(2)}) collective-permute-start(bf16[512,128]{1,0:T(8,128)(2,1)S(1)} %constant_dynamic-slice_fusion), channel_id=1, source_target_pairs={{0,48},{48,0},{1,49},{49,1},{2,50},{50,2},{3,51},{51,3},{4,52},{52... | collective-permute-start | bytes 393224 | tf_op jit(solution)/shard_map/ppermute | solution.py:23
  39.8 11.8 %collective-permute-start.5 = (bf16[2,512,128]{2,1,0:T(8,128)(2,1)S(1)}, bf16[2,512,128]{2,1,0:T(8,128)(2,1)S(1)}, u32[]{:S(2)}, u32[]{:S(2)}) collective-permute-start(bf16[2,512,128]{2,1,0:T(8,128)(2,1)S(1)} %maximum_select_fusion.1), channel_id=1, source_target_pairs={{0,96},{96,192},{192,288},{288,384},{384,480},{480,576},{576,672},... | collective-permute-start | bytes 786440 | tf_op jit(solution)/shard_map/ppermute | solution.py:33
  41.7 13.8 %collective-permute-start.10 = (bf16[2,512,128]{2,1,0:T(8,128)(2,1)S(1)}, bf16[2,512,128]{2,1,0:T(8,128)(2,1)S(1)}, u32[]{:S(2)}, u32[]{:S(2)}) collective-permute-start(bf16[2,512,128]{2,1,0:T(8,128)(2,1)S(1)} %get-tuple-element.28), channel_id=1, source_target_pairs={{0,96},{96,192},{192,288},{288,384},{384,480},{480,576},{576,672},... | collective-permute-start | bytes 786440 | tf_op jit(solution)/shard_map/ppermute | solution.py:48
  43.6 13.9 %collective-permute-start.2 = (bf16[2,512,128]{2,1,0:T(8,128)(2,1)S(1)}, bf16[2,512,128]{2,1,0:T(8,128)(2,1)S(1)}, u32[]{:S(2)}, u32[]{:S(2)}) collective-permute-start(bf16[2,512,128]{2,1,0:T(8,128)(2,1)S(1)} %maximum_select_fusion.1), channel_id=1, source_target_pairs={{0,672},{96,0},{192,96},{288,192},{384,288},{480,384},{576,480},{6... | collective-permute-start | bytes 786440 | tf_op jit(solution)/shard_map/ppermute | solution.py:37
  48.2 22.8 %collective-permute-start.14 = (bf16[2,512,128]{2,1,0:T(8,128)(2,1)S(1)}, bf16[2,512,128]{2,1,0:T(8,128)(2,1)S(1)}, u32[]{:S(2)}, u32[]{:S(2)}) collective-permute-start(bf16[2,512,128]{2,1,0:T(8,128)(2,1)S(1)} %get-tuple-element.29), channel_id=1, source_target_pairs={{0,672},{96,0},{192,96},{288,192},{384,288},{480,384},{576,480},{6... | collective-permute-start | bytes 786440 | tf_op jit(solution)/shard_map/ppermute | solution.py:54
  51.6 11.3 %collective-permute-start.6 = (bf16[2,512,128]{2,1,0:T(8,128)(2,1)S(1)}, bf16[2,512,128]{2,1,0:T(8,128)(2,1)S(1)}, u32[]{:S(2)}, u32[]{:S(2)}) collective-permute-start(bf16[2,512,128]{2,1,0:T(8,128)(2,1)S(1)} %collective-permute-done.5), channel_id=1, source_target_pairs={{0,96},{96,192},{192,288},{288,384},{384,480},{480,576},{576,672},... | collective-permute-start | bytes 786440 | tf_op jit(solution)/shard_map/ppermute | solution.py:33
  55.6 15.5 %collective-permute-start.11 = (bf16[2,512,128]{2,1,0:T(8,128)(2,1)S(1)}, bf16[2,512,128]{2,1,0:T(8,128)(2,1)S(1)}, u32[]{:S(2)}, u32[]{:S(2)}) collective-permute-start(bf16[2,512,128]{2,1,0:T(8,128)(2,1)S(1)} %fusion.21), channel_id=1, source_target_pairs={{0,96},{96,192},{192,288},{288,384},{384,480},{480,576},{576,672},... | collective-permute-start | bytes 786440 | tf_op jit(solution)/shard_map/ppermute | solution.py:48
  57.5 8.2 %collective-permute-start.3 = (bf16[2,512,128]{2,1,0:T(8,128)(2,1)S(1)}, bf16[2,512,128]{2,1,0:T(8,128)(2,1)S(1)}, u32[]{:S(2)}, u32[]{:S(2)}) collective-permute-start(bf16[2,512,128]{2,1,0:T(8,128)(2,1)S(1)} %collective-permute-done.2), channel_id=1, source_target_pairs={{0,672},{96,0},{192,96},{288,192},{384,288},{480,384},{576,480},{6... | collective-permute-start | bytes 786440 | tf_op jit(solution)/shard_map/ppermute | solution.py:37
  62.8 14.9 %collective-permute-start.7 = (bf16[2,512,128]{2,1,0:T(8,128)(2,1)S(1)}, bf16[2,512,128]{2,1,0:T(8,128)(2,1)S(1)}, u32[]{:S(2)}, u32[]{:S(2)}) collective-permute-start(bf16[2,512,128]{2,1,0:T(8,128)(2,1)S(1)} %collective-permute-done.6), channel_id=1, source_target_pairs={{0,96},{96,192},{192,288},{288,384},{384,480},{480,576},{576,672},... | collective-permute-start | bytes 786440 | tf_op jit(solution)/shard_map/ppermute | solution.py:33
  65.7 14.7 %collective-permute-start.4 = (bf16[2,512,128]{2,1,0:T(8,128)(2,1)S(1)}, bf16[2,512,128]{2,1,0:T(8,128)(2,1)S(1)}, u32[]{:S(2)}, u32[]{:S(2)}) collective-permute-start(bf16[2,512,128]{2,1,0:T(8,128)(2,1)S(1)} %collective-permute-done.3), channel_id=1, source_target_pairs={{0,672},{96,0},{192,96},{288,192},{384,288},{480,384},{576,480},{6... | collective-permute-start | bytes 786440 | tf_op jit(solution)/shard_map/ppermute | solution.py:37
  71.2 24.5 %collective-permute-start.12 = (bf16[2,512,128]{2,1,0:T(8,128)(2,1)S(1)}, bf16[2,512,128]{2,1,0:T(8,128)(2,1)S(1)}, u32[]{:S(2)}, u32[]{:S(2)}) collective-permute-start(bf16[2,512,128]{2,1,0:T(8,128)(2,1)S(1)} %get-tuple-element.26), channel_id=1, source_target_pairs={{0,96},{96,192},{192,288},{288,384},{384,480},{480,576},{576,672},... | collective-permute-start | bytes 786440 | tf_op jit(solution)/shard_map/ppermute | solution.py:48
  73.2 22.6 %collective-permute-start.15 = (bf16[2,512,128]{2,1,0:T(8,128)(2,1)S(1)}, bf16[2,512,128]{2,1,0:T(8,128)(2,1)S(1)}, u32[]{:S(2)}, u32[]{:S(2)}) collective-permute-start(bf16[2,512,128]{2,1,0:T(8,128)(2,1)S(1)} %get-tuple-element.27), channel_id=1, source_target_pairs={{0,672},{96,0},{192,96},{288,192},{384,288},{480,384},{576,480},{6... | collective-permute-start | bytes 786440 | tf_op jit(solution)/shard_map/ppermute | solution.py:54
  77.7 8.3 %collective-permute-start.8 = (bf16[2,512,128]{2,1,0:T(8,128)(2,1)S(1)}, bf16[2,512,128]{2,1,0:T(8,128)(2,1)S(1)}, u32[]{:S(2)}, u32[]{:S(2)}) collective-permute-start(bf16[2,512,128]{2,1,0:T(8,128)(2,1)S(1)} %collective-permute-done.7), channel_id=1, source_target_pairs={{0,96},{96,192},{192,288},{288,384},{384,480},{480,576},{576,672},... | collective-permute-start | bytes 786440 | tf_op jit(solution)/shard_map/ppermute | solution.py:33
  88.9 62.9 %collective-permute-start.9 = (bf16[8,2,512,128]{3,2,1,0:T(8,128)(2,1)}, bf16[8,2,512,128]{3,2,1,0:T(8,128)(2,1)}, u32[]{:S(2)}, u32[]{:S(2)}) collective-permute-start(bf16[8,2,512,128]{3,2,1,0:T(8,128)(2,1)} %bitcast_dynamic-update-slice_fusion), channel_id=1, source_target_pairs={{0,1},{1,0},{2,3},{3,2},{4,5},{5,4},{6,7},{7,6},{8,9},{9,8},{10,11... | collective-permute-start | bytes 6291464 | tf_op jit(solution)/shard_map/ppermute | solution.py:123
  95.9 11.0 %collective-permute-start.13 = (bf16[2,512,128]{2,1,0:T(8,128)(2,1)S(1)}, bf16[2,512,128]{2,1,0:T(8,128)(2,1)S(1)}, u32[]{:S(2)}, u32[]{:S(2)}) collective-permute-start(bf16[2,512,128]{2,1,0:T(8,128)(2,1)S(1)} %get-tuple-element.24), channel_id=1, source_target_pairs={{0,96},{96,192},{192,288},{288,384},{384,480},{480,576},{576,672},... | collective-permute-start | bytes 786440 | tf_op jit(solution)/shard_map/ppermute | solution.py:50
  97.8 29.0 %copy-start.6 = (bf16[256,2048]{1,0:T(8,128)(2,1)S(1)}, bf16[256,2048]{1,0:T(8,128)(2,1)}, u32[]{:S(2)}) copy-start(bf16[256,2048]{1,0:T(8,128)(2,1)} %param.13) | copy-start | bytes 3145732
  97.8 10.1 %collective-permute-start.16 = (bf16[2,512,128]{2,1,0:T(8,128)(2,1)S(1)}, bf16[2,512,128]{2,1,0:T(8,128)(2,1)S(1)}, u32[]{:S(2)}, u32[]{:S(2)}) collective-permute-start(bf16[2,512,128]{2,1,0:T(8,128)(2,1)S(1)} %get-tuple-element.25), channel_id=1, source_target_pairs={{0,672},{96,0},{192,96},{288,192},{384,288},{480,384},{576,480},{6... | collective-permute-start | bytes 786440 | tf_op jit(solution)/shard_map/ppermute | solution.py:56
  108.1 8.6 %collective-permute-start.17 = (f32[512,128]{1,0:T(8,128)S(1)}, f32[512,128]{1,0:T(8,128)S(1)}, u32[]{:S(2)}, u32[]{:S(2)}) collective-permute-start(f32[512,128]{1,0:T(8,128)S(1)} %select_bitcast_fusion), channel_id=1, source_target_pairs={{0,48},{48,0},{1,49},{49,1},{2,50},{50,2},{3,51},{51,3},{4,52},{52... | collective-permute-start | bytes 786440 | tf_op jit(solution)/shard_map/ppermute | solution.py:141
  117.4 22.4 %all-to-all-start = ((f32[24,22,128]{2,1,0:T(8,128)}), f32[24,22,128]{2,1,0:T(8,128)S(1)}, u32[]{:S(2)}, u32[]{:S(2)}) async-start(f32[24,22,128]{2,1,0:T(8,128)} %reshape.341), calls=%async_computation | async-start | bytes 589824 | tf_op jit(solution)/shard_map/all_to_all | solution.py:145
  140.7 39.8 %all-to-all-start.1 = ((f32[48,22,128]{2,1,0:T(8,128)}), f32[48,22,128]{2,1,0:T(8,128)S(1)}, u32[]{:S(2)}, u32[]{:S(2)}) async-start(f32[48,22,128]{2,1,0:T(8,128)} %broadcast_in_dim.12), calls=%async_computation.1 | async-start | bytes 1179648 | tf_op jit(solution)/shard_map/all_to_all | solution.py:149
  (6 other events, 12.2 us)

commit v6 on v5

--- a/solution.py
+++ b/solution.py
@@ -142,6 +142,8 @@
     groups = lax.axis_size("rz")
     piece_rows = -(-part_rows // groups)
     padded = jnp.pad(shard_sum, ((0, piece_rows * groups - part_rows), (0, 0)))
+    padded, grad_att = lax.optimization_barrier((padded, grad_att))
+    grad_h = grad_att.reshape(seq_count, SEQ, HEADS, HEAD_DIM)
     pieces = lax.all_to_all(
         padded.reshape(groups, piece_rows, -1), "rz", 0, 0, tiled=True
     )

time: 184 us -> 194 us (1.054)
  waiting for transfers between devices: 48.9 us -> 55.5 us
  local copies, waits for them, and re-layouts: 17.1 us -> 20.5 us
    ppermute x4, waiting for transfers between devices: 4.95 us -> 10.2 us  [ring_gather(): moving = lax.ppermute(moving, 'y', right)]
    ppermute x1, waiting for transfers between devices: 4.38 us -> 0.01 us  [ring_reduce(): from_left = lax.ppermute(moving, 'y', right)]
    all_to_all x1, waiting for transfers between devices: 15.6 us -> 18.8 us  [local(): lax.all_to_all(jnp.broadcast_to(piece_sum[None], (groups * cores,) + piec...]
    all_to_all x1, waiting for transfers between devices: 9.44 us -> 12.5 us  [local(): lax.all_to_all(padded.reshape(groups, piece_rows, -1), 'rz', 0, 0, tiled=...]
    ppermute x1, waiting for transfers between devices: 6.22 us -> 3.17 us  [local(): shard_sum = keep + lax.ppermute(send, 'xl', [(0, 1), (1, 0)])]
    ppermute x3, waiting for transfers between devices: 2.02 us -> 4.9 us  [ring_reduce(): moving = lax.ppermute(moving, 'y', right)]
where the time goes in v6:
time: 194 us; the launch traced here: 193 us
  starting transfers between devices  87.5 us (45%)
  waiting for transfers between devices  55.5 us (29%)
  local copies, waits for them, and re-layouts  20.5 us (11%)
  matrix products  17.4 us (9%)
  other arithmetic  11.2 us (6%)
    all_to_all x1, waiting for transfers between devices, local(): lax.all_to_all(jnp.broadcast_to(piece_sum[None], (groups * cores,) + piec...  18.8 us
    ppermute x3, starting transfers between devices, ring_gather(): moving = lax.ppermute(moving, 'y', left)  13.7 us
    all_to_all x1, waiting for transfers between devices, local(): lax.all_to_all(padded.reshape(groups, piece_rows, -1), 'rz', 0, 0, tiled=...  12.5 us
    ppermute x1, starting transfers between devices, local(): got_half = lax.ppermute(sent_half, 'core', [(0, 1), (1, 0)])  12.4 us
    unnamed x33, local copies, waits for them, and re-layouts  11.6 us
    all_to_all x1, starting transfers between devices, local(): lax.all_to_all(jnp.broadcast_to(piece_sum[None], (groups * cores,) + piec...  11.1 us
    all_to_all x1, starting transfers between devices, local(): lax.all_to_all(padded.reshape(groups, piece_rows, -1), 'rz', 0, 0, tiled=...  10.8 us
    ppermute x4, waiting for transfers between devices, ring_gather(): moving = lax.ppermute(moving, 'y', right)  10.2 us
  transfers between devices with their start and end apart: 20, of which 9 were waited for; matrix products, arithmetic and copies ran while one was open for 13% of the time, Pallas kernels for 0%

profile of v6, /device:TPU:1, one launch (start us, length us, event | category | flops | bytes accessed | tf_op | source)
XLA Modules:
  0.0 193.3 jit_solution(13887146544733846047)
XLA Ops:
  10.0 3.2 %multiply_convert_fusion = bf16[1024,16,128]{2,0,1:T(8,128)(2,1)} fusion(bf16[256,1024,1]{0,1,2:T(8,128)(2,1)S(1)} %bitcast.167, bf16[256,2048]{1,0:T(8,128)(2,1)S(1)} %copy-done.5), kind=kOutput, calls=%fused_computation.1 | convolution fusion | flops 1077936128 | bytes 5767168 | tf_op jit(solution)/shard_map/tr,tjc->jrc/dot_general | solution.py:107
  13.3 2.5 %fusion.2 = bf16[16,512,128]{2,1,0:T(8,128)(2,1)S(1)} fusion(pred[]{:T(512)S(6)} %eq.87, bf16[16,2,512,128]{3,2,1,0:T(8,128)(2,1)} %bitcast.153), kind=kLoop, calls=%fused_computation.7 | loop fusion | flops 1048576 | bytes 6291457 | tf_op jit(solution)/shard_map/jit(_where)/select_n | solution.py:117
  15.8 12.4 %collective-permute-start.1 = (bf16[16,512,128]{2,1,0:T(8,128)(2,1)S(1)}, bf16[16,512,128]{2,1,0:T(8,128)(2,1)}, u32[]{:S(2)}, u32[]{:S(2)}) collective-permute-start(bf16[16,512,128]{2,1,0:T(8,128)(2,1)S(1)} %fusion.2), channel_id=1, source_target_pairs={{0,1},{1,0},{2,3},{3,2},{4,5},{5,4},{6,7},{7,6},{8,9},{9,8},{10,11... | collective-permute-start | bytes 6291464 | tf_op jit(solution)/shard_map/ppermute | solution.py:118
  30.2 5.0 %collective-permute-done = bf16[512,128]{1,0:T(8,128)(2,1)S(1)} collective-permute-done((bf16[512,128]{1,0:T(8,128)(2,1)S(1)}, bf16[512,128]{1,0:T(8,128)(2,1)S(1)}, u32[]{:S(2)}, u32[]{:S(2)}) %collective-permute-start) | collective-permute-done | bytes 131104 | tf_op jit(solution)/shard_map/ppermute | solution.py:23
  35.3 3.7 %fusion.1 = bf16[16,512,128]{2,1,0:T(8,128)(2,1)S(1)} fusion(bf16[16,512,128]{2,1,0:T(8,128)(2,1)} %collective-permute-done.1, pred[]{:T(512)S(6)} %eq.87, bf16[16,2,512,128]{3,2,1,0:T(8,128)(2,1)} %bitcast.154), kind=kLoop, calls=%fused_computation.5 | loop fusion | flops 5242880 | bytes 8388609 | tf_op jit(solution)/shard_map/convert_element_type | solution.py:119
  41.7 4.6 %collective-permute-start.10 = (bf16[2,512,128]{2,1,0:T(8,128)(2,1)S(1)}, bf16[2,512,128]{2,1,0:T(8,128)(2,1)S(1)}, u32[]{:S(2)}, u32[]{:S(2)}) collective-permute-start(bf16[2,512,128]{2,1,0:T(8,128)(2,1)S(1)} %maximum_select_fusion.1), channel_id=1, source_target_pairs={{0,672},{96,0},{192,96},{288,192},{384,288},{480,384},{576,480},{6... | collective-permute-start | bytes 786440 | tf_op jit(solution)/shard_map/ppermute | solution.py:37
  46.3 3.6 %collective-permute-done.13 = bf16[2,512,128]{2,1,0:T(8,128)(2,1)S(1)} collective-permute-done((bf16[2,512,128]{2,1,0:T(8,128)(2,1)S(1)}, bf16[2,512,128]{2,1,0:T(8,128)(2,1)S(1)}, u32[]{:S(2)}, u32[]{:S(2)}) %collective-permute-start.13) | collective-permute-done | bytes 262176 | tf_op jit(solution)/shard_map/ppermute | solution.py:33
  53.7 4.6 %collective-permute-start.11 = (bf16[2,512,128]{2,1,0:T(8,128)(2,1)S(1)}, bf16[2,512,128]{2,1,0:T(8,128)(2,1)S(1)}, u32[]{:S(2)}, u32[]{:S(2)}) collective-permute-start(bf16[2,512,128]{2,1,0:T(8,128)(2,1)S(1)} %collective-permute-done.10), channel_id=1, source_target_pairs={{0,672},{96,0},{192,96},{288,192},{384,288},{480,384},{576,480},{6... | collective-permute-start | bytes 786440 | tf_op jit(solution)/shard_map/ppermute | solution.py:37
  59.0 3.4 %collective-permute-start.6 = (bf16[2,512,128]{2,1,0:T(8,128)(2,1)S(1)}, bf16[2,512,128]{2,1,0:T(8,128)(2,1)S(1)}, u32[]{:S(2)}, u32[]{:S(2)}) collective-permute-start(bf16[2,512,128]{2,1,0:T(8,128)(2,1)S(1)} %get-tuple-element.33), channel_id=1, source_target_pairs={{0,672},{96,0},{192,96},{288,192},{384,288},{480,384},{576,480},{6... | collective-permute-start | bytes 786440 | tf_op jit(solution)/shard_map/ppermute | solution.py:54
  66.7 4.6 %collective-permute-start.12 = (bf16[2,512,128]{2,1,0:T(8,128)(2,1)S(1)}, bf16[2,512,128]{2,1,0:T(8,128)(2,1)S(1)}, u32[]{:S(2)}, u32[]{:S(2)}) collective-permute-start(bf16[2,512,128]{2,1,0:T(8,128)(2,1)S(1)} %collective-permute-done.11), channel_id=1, source_target_pairs={{0,672},{96,0},{192,96},{288,192},{384,288},{480,384},{576,480},{6... | collective-permute-start | bytes 786440 | tf_op jit(solution)/shard_map/ppermute | solution.py:37
  75.4 6.6 %collective-permute-done.16 = bf16[2,512,128]{2,1,0:T(8,128)(2,1)S(1)} collective-permute-done((bf16[2,512,128]{2,1,0:T(8,128)(2,1)S(1)}, bf16[2,512,128]{2,1,0:T(8,128)(2,1)S(1)}, u32[]{:S(2)}, u32[]{:S(2)}) %collective-permute-start.16) | collective-permute-done | bytes 262176 | tf_op jit(solution)/shard_map/ppermute | solution.py:33
  84.8 6.4 %collective-permute-start.17 = (bf16[8,2,512,128]{3,2,1,0:T(8,128)(2,1)}, bf16[8,2,512,128]{3,2,1,0:T(8,128)(2,1)}, u32[]{:S(2)}, u32[]{:S(2)}) collective-permute-start(bf16[8,2,512,128]{3,2,1,0:T(8,128)(2,1)} %bitcast_dynamic-update-slice_fusion), channel_id=1, source_target_pairs={{0,1},{1,0},{2,3},{3,2},{4,5},{5,4},{6,7},{7,6},{8,9},{9,8},{10,11... | collective-permute-start | bytes 6291464 | tf_op jit(solution)/shard_map/ppermute | solution.py:123
  93.3 4.6 %collective-permute-start.7 = (bf16[2,512,128]{2,1,0:T(8,128)(2,1)S(1)}, bf16[2,512,128]{2,1,0:T(8,128)(2,1)S(1)}, u32[]{:S(2)}, u32[]{:S(2)}) collective-permute-start(bf16[2,512,128]{2,1,0:T(8,128)(2,1)S(1)} %get-tuple-element.31), channel_id=1, source_target_pairs={{0,672},{96,0},{192,96},{288,192},{384,288},{480,384},{576,480},{6... | collective-permute-start | bytes 786440 | tf_op jit(solution)/shard_map/ppermute | solution.py:54
  97.9 4.5 %collective-permute-done.4 = bf16[2,512,128]{2,1,0:T(8,128)(2,1)S(1)} collective-permute-done((bf16[2,512,128]{2,1,0:T(8,128)(2,1)S(1)}, bf16[2,512,128]{2,1,0:T(8,128)(2,1)S(1)}, u32[]{:S(2)}, u32[]{:S(2)}) %collective-permute-start.4) | collective-permute-done | bytes 262176 | tf_op jit(solution)/shard_map/ppermute | solution.py:48
  106.1 5.3 %collective-permute-start.8 = (bf16[2,512,128]{2,1,0:T(8,128)(2,1)S(1)}, bf16[2,512,128]{2,1,0:T(8,128)(2,1)S(1)}, u32[]{:S(2)}, u32[]{:S(2)}) collective-permute-start(bf16[2,512,128]{2,1,0:T(8,128)(2,1)S(1)} %get-tuple-element.29), channel_id=1, source_target_pairs={{0,672},{96,0},{192,96},{288,192},{384,288},{480,384},{576,480},{6... | collective-permute-start | bytes 786440 | tf_op jit(solution)/shard_map/ppermute | solution.py:56
  113.7 2.3 %copy.93 = bf16[256,8,2,128]{3,0,2,1:T(8,128)(2,1)} copy(bf16[256,8,2,128]{0,3,2,1:T(8,128)(2,1)} %bitcast.157) | data formatting | bytes 2097152 | tf_op jit(solution)/shard_map/reshape | solution.py:124
  116.1 2.5 %collective-permute-start.9 = (f32[512,128]{1,0:T(8,128)S(1)}, f32[512,128]{1,0:T(8,128)S(1)}, u32[]{:S(2)}, u32[]{:S(2)}) collective-permute-start(f32[512,128]{1,0:T(8,128)S(1)} %select_bitcast_fusion), channel_id=1, source_target_pairs={{0,48},{48,0},{1,49},{49,1},{2,50},{50,2},{3,51},{51,3},{4,52},{52... | collective-permute-start | bytes 786440 | tf_op jit(solution)/shard_map/ppermute | solution.py:141
  118.6 2.4 %convolution_bitcast_fusion.1 = bf16[256,512]{1,0:T(8,128)(2,1)S(1)} fusion(bf16[8,2,512,128]{3,2,1,0:T(8,128)(2,1)} %bitcast_dynamic-update-slice_fusion, s32[]{:T(128)S(6)} %select_n.87, bf16[256,8,2,128]{3,0,2,1:T(8,128)(2,1)S(1)} %copy-done.6), kind=kOutput, calls=%fused_computation.22 | convolution fusion | flops 537395200 | bytes 3407876 | tf_op jit(solution)/shard_map/toxc,oxrc->tr/dot_general | solution.py:125
  121.0 3.2 %collective-permute-done.9 = f32[512,128]{1,0:T(8,128)S(1)} collective-permute-done((f32[512,128]{1,0:T(8,128)S(1)}, f32[512,128]{1,0:T(8,128)S(1)}, u32[]{:S(2)}, u32[]{:S(2)}) %collective-permute-start.9) | collective-permute-done | bytes 262176 | tf_op jit(solution)/shard_map/ppermute | solution.py:141
  124.3 2.4 %convolution_bitcast_fusion = bf16[256,512]{1,0:T(8,128)(2,1)S(1)} fusion(bf16[8,2,512,128]{3,2,1,0:T(8,128)(2,1)} %collective-permute-done.17, s32[]{:T(128)S(6)} %select_n.87, bf16[256,8,2,128]{3,0,2,1:T(8,128)(2,1)S(1)} %copy-done.6), kind=kOutput, calls=%fused_computation.21 | convolution fusion | flops 537395200 | bytes 3407876 | tf_op jit(solution)/shard_map/toxc,oxrc->tr/dot_general | solution.py:128
  127.5 10.8 %all-to-all-start = ((f32[24,22,128]{2,1,0:T(8,128)}), f32[24,22,128]{2,1,0:T(8,128)S(1)}, u32[]{:S(2)}, u32[]{:S(2)}) async-start(f32[24,22,128]{2,1,0:T(8,128)} %reshape.336), calls=%async_computation | async-start | bytes 589824 | tf_op jit(solution)/shard_map/all_to_all | solution.py:147
  138.8 12.5 %all-to-all-done = f32[24,22,128]{2,1,0:T(8,128)S(1)} async-done(((f32[24,22,128]{2,1,0:T(8,128)}), f32[24,22,128]{2,1,0:T(8,128)S(1)}, u32[]{:S(2)}, u32[]{:S(2)}) %all-to-all-start) | async-done | bytes 270368 | tf_op jit(solution)/shard_map/all_to_all | solution.py:147
  152.2 11.1 %all-to-all-start.1 = ((f32[48,22,128]{2,1,0:T(8,128)}), f32[48,22,128]{2,1,0:T(8,128)S(1)}, u32[]{:S(2)}, u32[]{:S(2)}) async-start(f32[48,22,128]{2,1,0:T(8,128)} %broadcast_in_dim.12), calls=%async_computation.1 | async-start | bytes 1179648 | tf_op jit(solution)/shard_map/all_to_all | solution.py:151
  173.3 18.8 %all-to-all-done.1 = f32[48,22,128]{2,1,0:T(8,128)S(1)} async-done(((f32[48,22,128]{2,1,0:T(8,128)}), f32[48,22,128]{2,1,0:T(8,128)S(1)}, u32[]{:S(2)}, u32[]{:S(2)}) %all-to-all-start.1) | async-done | bytes 540704 | tf_op jit(solution)/shard_map/all_to_all | solution.py:151
  (90 shorter events, 51.2 us)
Async XLA Ops:
  0.6 6.5 %copy-start = (bf16[256,1024]{1,0:T(8,128)(2,1)S(1)}, bf16[256,1024]{1,0:T(8,128)(2,1)}, u32[]{:S(2)}) copy-start(bf16[256,1024]{1,0:T(8,128)(2,1)} %param.9) | copy-start | bytes 1572868
  3.3 3.8 %copy-start.1 = (bf16[256,1024]{0,1:T(8,128)(2,1)}, bf16[256,1024]{0,1:T(8,128)(2,1)S(1)}, u32[]{:S(2)}) copy-start(bf16[256,1024]{0,1:T(8,128)(2,1)S(1)} %copy.124) | copy-start | bytes 1572868
  13.3 14.9 %copy-start.9 = (bf16[1024,128]{1,0:T(8,128)(2,1)S(1)}, bf16[1024,128]{1,0:T(8,128)(2,1)}, u32[]{:S(2)}) copy-start(bf16[1024,128]{1,0:T(8,128)(2,1)} %param.12) | copy-start | bytes 786436
  15.8 19.5 %collective-permute-start.1 = (bf16[16,512,128]{2,1,0:T(8,128)(2,1)S(1)}, bf16[16,512,128]{2,1,0:T(8,128)(2,1)}, u32[]{:S(2)}, u32[]{:S(2)}) collective-permute-start(bf16[16,512,128]{2,1,0:T(8,128)(2,1)S(1)} %fusion.2), channel_id=1, source_target_pairs={{0,1},{1,0},{2,3},{3,2},{4,5},{5,4},{6,7},{7,6},{8,9},{9,8},{10,11... | collective-permute-start | bytes 6291464 | tf_op jit(solution)/shard_map/ppermute | solution.py:118
  28.2 7.0 %collective-permute-start = (bf16[512,128]{1,0:T(8,128)(2,1)S(1)}, bf16[512,128]{1,0:T(8,128)(2,1)S(1)}, u32[]{:S(2)}, u32[]{:S(2)}) collective-permute-start(bf16[512,128]{1,0:T(8,128)(2,1)S(1)} %constant_dynamic-slice_fusion), channel_id=1, source_target_pairs={{0,48},{48,0},{1,49},{49,1},{2,50},{50,2},{3,51},{51,3},{4,52},{52... | collective-permute-start | bytes 393224 | tf_op jit(solution)/shard_map/ppermute | solution.py:23
  39.7 10.1 %collective-permute-start.13 = (bf16[2,512,128]{2,1,0:T(8,128)(2,1)S(1)}, bf16[2,512,128]{2,1,0:T(8,128)(2,1)S(1)}, u32[]{:S(2)}, u32[]{:S(2)}) collective-permute-start(bf16[2,512,128]{2,1,0:T(8,128)(2,1)S(1)} %maximum_select_fusion.1), channel_id=1, source_target_pairs={{0,96},{96,192},{192,288},{288,384},{384,480},{480,576},{576,672},... | collective-permute-start | bytes 786440 | tf_op jit(solution)/shard_map/ppermute | solution.py:33
  41.7 12.1 %collective-permute-start.10 = (bf16[2,512,128]{2,1,0:T(8,128)(2,1)S(1)}, bf16[2,512,128]{2,1,0:T(8,128)(2,1)S(1)}, u32[]{:S(2)}, u32[]{:S(2)}) collective-permute-start(bf16[2,512,128]{2,1,0:T(8,128)(2,1)S(1)} %maximum_select_fusion.1), channel_id=1, source_target_pairs={{0,672},{96,0},{192,96},{288,192},{384,288},{480,384},{576,480},{6... | collective-permute-start | bytes 786440 | tf_op jit(solution)/shard_map/ppermute | solution.py:37
  49.9 12.5 %collective-permute-start.14 = (bf16[2,512,128]{2,1,0:T(8,128)(2,1)S(1)}, bf16[2,512,128]{2,1,0:T(8,128)(2,1)S(1)}, u32[]{:S(2)}, u32[]{:S(2)}) collective-permute-start(bf16[2,512,128]{2,1,0:T(8,128)(2,1)S(1)} %collective-permute-done.13), channel_id=1, source_target_pairs={{0,96},{96,192},{192,288},{288,384},{384,480},{480,576},{576,672},... | collective-permute-start | bytes 786440 | tf_op jit(solution)/shard_map/ppermute | solution.py:33
  51.8 12.9 %collective-permute-start.2 = (bf16[2,512,128]{2,1,0:T(8,128)(2,1)S(1)}, bf16[2,512,128]{2,1,0:T(8,128)(2,1)S(1)}, u32[]{:S(2)}, u32[]{:S(2)}) collective-permute-start(bf16[2,512,128]{2,1,0:T(8,128)(2,1)S(1)} %get-tuple-element.32), channel_id=1, source_target_pairs={{0,96},{96,192},{192,288},{288,384},{384,480},{480,576},{576,672},... | collective-permute-start | bytes 786440 | tf_op jit(solution)/shard_map/ppermute | solution.py:48
  53.7 13.0 %collective-permute-start.11 = (bf16[2,512,128]{2,1,0:T(8,128)(2,1)S(1)}, bf16[2,512,128]{2,1,0:T(8,128)(2,1)S(1)}, u32[]{:S(2)}, u32[]{:S(2)}) collective-permute-start(bf16[2,512,128]{2,1,0:T(8,128)(2,1)S(1)} %collective-permute-done.10), channel_id=1, source_target_pairs={{0,672},{96,0},{192,96},{288,192},{384,288},{480,384},{576,480},{6... | collective-permute-start | bytes 786440 | tf_op jit(solution)/shard_map/ppermute | solution.py:37
  59.0 32.2 %collective-permute-start.6 = (bf16[2,512,128]{2,1,0:T(8,128)(2,1)S(1)}, bf16[2,512,128]{2,1,0:T(8,128)(2,1)S(1)}, u32[]{:S(2)}, u32[]{:S(2)}) collective-permute-start(bf16[2,512,128]{2,1,0:T(8,128)(2,1)S(1)} %get-tuple-element.33), channel_id=1, source_target_pairs={{0,672},{96,0},{192,96},{288,192},{384,288},{480,384},{576,480},{6... | collective-permute-start | bytes 786440 | tf_op jit(solution)/shard_map/ppermute | solution.py:54
  62.4 9.6 %collective-permute-start.15 = (bf16[2,512,128]{2,1,0:T(8,128)(2,1)S(1)}, bf16[2,512,128]{2,1,0:T(8,128)(2,1)S(1)}, u32[]{:S(2)}, u32[]{:S(2)}) collective-permute-start(bf16[2,512,128]{2,1,0:T(8,128)(2,1)S(1)} %collective-permute-done.14), channel_id=1, source_target_pairs={{0,96},{96,192},{192,288},{288,384},{384,480},{480,576},{576,672},... | collective-permute-start | bytes 786440 | tf_op jit(solution)/shard_map/ppermute | solution.py:33
  64.8 26.5 %collective-permute-start.3 = (bf16[2,512,128]{2,1,0:T(8,128)(2,1)S(1)}, bf16[2,512,128]{2,1,0:T(8,128)(2,1)S(1)}, u32[]{:S(2)}, u32[]{:S(2)}) collective-permute-start(bf16[2,512,128]{2,1,0:T(8,128)(2,1)S(1)} %fusion.20), channel_id=1, source_target_pairs={{0,96},{96,192},{192,288},{288,384},{384,480},{480,576},{576,672},... | collective-permute-start | bytes 786440 | tf_op jit(solution)/shard_map/ppermute | solution.py:48
  66.7 8.0 %collective-permute-start.12 = (bf16[2,512,128]{2,1,0:T(8,128)(2,1)S(1)}, bf16[2,512,128]{2,1,0:T(8,128)(2,1)S(1)}, u32[]{:S(2)}, u32[]{:S(2)}) collective-permute-start(bf16[2,512,128]{2,1,0:T(8,128)(2,1)S(1)} %collective-permute-done.11), channel_id=1, source_target_pairs={{0,672},{96,0},{192,96},{288,192},{384,288},{480,384},{576,480},{6... | collective-permute-start | bytes 786440 | tf_op jit(solution)/shard_map/ppermute | solution.py:37
  72.0 9.9 %collective-permute-start.16 = (bf16[2,512,128]{2,1,0:T(8,128)(2,1)S(1)}, bf16[2,512,128]{2,1,0:T(8,128)(2,1)S(1)}, u32[]{:S(2)}, u32[]{:S(2)}) collective-permute-start(bf16[2,512,128]{2,1,0:T(8,128)(2,1)S(1)} %collective-permute-done.15), channel_id=1, source_target_pairs={{0,96},{96,192},{192,288},{288,384},{384,480},{480,576},{576,672},... | collective-permute-start | bytes 786440 | tf_op jit(solution)/shard_map/ppermute | solution.py:33
  84.8 39.5 %collective-permute-start.17 = (bf16[8,2,512,128]{3,2,1,0:T(8,128)(2,1)}, bf16[8,2,512,128]{3,2,1,0:T(8,128)(2,1)}, u32[]{:S(2)}, u32[]{:S(2)}) collective-permute-start(bf16[8,2,512,128]{3,2,1,0:T(8,128)(2,1)} %bitcast_dynamic-update-slice_fusion), channel_id=1, source_target_pairs={{0,1},{1,0},{2,3},{3,2},{4,5},{5,4},{6,7},{7,6},{8,9},{9,8},{10,11... | collective-permute-start | bytes 6291464 | tf_op jit(solution)/shard_map/ppermute | solution.py:123
  91.4 11.0 %collective-permute-start.4 = (bf16[2,512,128]{2,1,0:T(8,128)(2,1)S(1)}, bf16[2,512,128]{2,1,0:T(8,128)(2,1)S(1)}, u32[]{:S(2)}, u32[]{:S(2)}) collective-permute-start(bf16[2,512,128]{2,1,0:T(8,128)(2,1)S(1)} %get-tuple-element.30), channel_id=1, source_target_pairs={{0,96},{96,192},{192,288},{288,384},{384,480},{480,576},{576,672},... | collective-permute-start | bytes 786440 | tf_op jit(solution)/shard_map/ppermute | solution.py:48
  93.3 10.0 %collective-permute-start.7 = (bf16[2,512,128]{2,1,0:T(8,128)(2,1)S(1)}, bf16[2,512,128]{2,1,0:T(8,128)(2,1)S(1)}, u32[]{:S(2)}, u32[]{:S(2)}) collective-permute-start(bf16[2,512,128]{2,1,0:T(8,128)(2,1)S(1)} %get-tuple-element.31), channel_id=1, source_target_pairs={{0,672},{96,0},{192,96},{288,192},{384,288},{480,384},{576,480},{6... | collective-permute-start | bytes 786440 | tf_op jit(solution)/shard_map/ppermute | solution.py:54
  104.2 11.8 %collective-permute-start.5 = (bf16[2,512,128]{2,1,0:T(8,128)(2,1)}, bf16[2,512,128]{2,1,0:T(8,128)(2,1)S(1)}, u32[]{:S(2)}, u32[]{:S(2)}) collective-permute-start(bf16[2,512,128]{2,1,0:T(8,128)(2,1)} %get-tuple-element.28), channel_id=1, source_target_pairs={{0,96},{96,192},{192,288},{288,384},{384,480},{480,576},{576,672},... | collective-permute-start | bytes 786440 | tf_op jit(solution)/shard_map/ppermute | solution.py:50
  106.1 9.9 %collective-permute-start.8 = (bf16[2,512,128]{2,1,0:T(8,128)(2,1)S(1)}, bf16[2,512,128]{2,1,0:T(8,128)(2,1)S(1)}, u32[]{:S(2)}, u32[]{:S(2)}) collective-permute-start(bf16[2,512,128]{2,1,0:T(8,128)(2,1)S(1)} %get-tuple-element.29), channel_id=1, source_target_pairs={{0,672},{96,0},{192,96},{288,192},{384,288},{480,384},{576,480},{6... | collective-permute-start | bytes 786440 | tf_op jit(solution)/shard_map/ppermute | solution.py:56
  116.1 8.1 %collective-permute-start.9 = (f32[512,128]{1,0:T(8,128)S(1)}, f32[512,128]{1,0:T(8,128)S(1)}, u32[]{:S(2)}, u32[]{:S(2)}) collective-permute-start(f32[512,128]{1,0:T(8,128)S(1)} %select_bitcast_fusion), channel_id=1, source_target_pairs={{0,48},{48,0},{1,49},{49,1},{2,50},{50,2},{3,51},{51,3},{4,52},{52... | collective-permute-start | bytes 786440 | tf_op jit(solution)/shard_map/ppermute | solution.py:141
  127.5 23.8 %all-to-all-start = ((f32[24,22,128]{2,1,0:T(8,128)}), f32[24,22,128]{2,1,0:T(8,128)S(1)}, u32[]{:S(2)}, u32[]{:S(2)}) async-start(f32[24,22,128]{2,1,0:T(8,128)} %reshape.336), calls=%async_computation | async-start | bytes 589824 | tf_op jit(solution)/shard_map/all_to_all | solution.py:147
  138.8 26.7 %copy-start.8 = (bf16[256,8,128]{0,2,1:T(8,128)(2,1)}, bf16[256,8,128]{0,2,1:T(8,128)(2,1)S(1)}, u32[]{:S(2)}) copy-start(bf16[256,8,128]{0,2,1:T(8,128)(2,1)S(1)} %copy.102) | copy-start | bytes 1572868
  152.2 39.8 %all-to-all-start.1 = ((f32[48,22,128]{2,1,0:T(8,128)}), f32[48,22,128]{2,1,0:T(8,128)S(1)}, u32[]{:S(2)}, u32[]{:S(2)}) async-start(f32[48,22,128]{2,1,0:T(8,128)} %broadcast_in_dim.12), calls=%async_computation.1 | async-start | bytes 1179648 | tf_op jit(solution)/shard_map/all_to_all | solution.py:151
  (6 other events, 12.5 us)
